TPU v7x, 256 devices: a whole 4x4x8 slice. The times are simulated.
256 devices in a mesh: seq: 64 (over z, y, core), mp: 4 (over x).
Axes of the slice: x: 4, y: 4, z: 8, core: 2. Of those that a mesh axis runs over, the one named last changes fastest.
Arguments:
- patches: bfloat16 [262144, 1280], P('seq'), may hold values from -2 to 2
- w_qkv: bfloat16 [1280, 3840], P('seq', 'mp'), as said below
- w_out: bfloat16 [1280, 1280], P('mp', 'seq'), may hold values from -0.15625 to 0.15625
- page_rows: int32 [64], replicated, may hold values from 32 to 64, as said below
- page_cols: int32 [64], replicated, may hold values from 32 to 64, as said below
- window_slot: int32 [64, 64], replicated, may hold values from 0 to 63, each once within a row
Outputs:
- blocks: bfloat16 [262144, 1280], P('seq', 'mp')
Inputs may be any that keep to these rules, and one draw needn't show every extreme that they name: `page_rows`: page heights, multiples of 16; some page has the largest. `page_cols`: page widths, multiples of 16; some page has the largest. `window_slot`: each row is a permutation. `w_qkv`: entries of order at most 5.5 / sqrt(1280).
All inputs are finite; a program needn't handle non-finite values.
Results may differ from a plain program's by a relative error of at most 0.012.
Values may be sent and summed in bfloat16 or wider, within the bound.
No kernel may reach another device: no remote copies, remote signals or barrier semaphores. Data moves between devices by JAX's collectives and lax.ppermute only.
A program may use at most 192 MiB of HBM per device.

v0:
```python
import math

import jax
import jax.numpy as jnp
from jax import lax
from jax.sharding import PartitionSpec as P

HD = 80
WS = 8


EPSILON = 1e-06


def rotate(vector, cosine_table, sine_table):
    half_size = vector.shape[-1] // 2
    turned = jnp.concatenate([-vector[..., half_size:], vector[..., :half_size]], axis=-1)
    return vector * cosine_table + turned * sine_table


def angle_tables(row_place, column_place, head_size):
    quarter = head_size // 4
    frequency = 1.0 / 10000.0 ** (jnp.arange(quarter, dtype=jnp.float32) * 2.0 / (head_size // 2))
    angles = jnp.concatenate(
        [
            row_place[..., None].astype(jnp.float32) * frequency,
            column_place[..., None].astype(jnp.float32) * frequency,
        ],
        axis=-1,
    )
    angles = jnp.concatenate([angles, angles], axis=-1)
    return (jnp.cos(angles), jnp.sin(angles))


def slot_positions(page_widths, slot_table, slot_numbers, window_side):
    matches = slot_table[:, :, None] == slot_numbers[None, None, :]
    ordinal = jnp.arange(slot_table.shape[1], dtype=jnp.int32)
    window = jnp.sum(jnp.where(matches, ordinal[None, :, None], 0), axis=1)
    across = page_widths // window_side
    window_row = window // across[:, None]
    window_column = window % across[:, None]
    unit_side = window_side // 2
    position = jnp.arange(window_side * window_side, dtype=jnp.int32)
    merge_unit = position // 4
    corner = position % 4
    inner_row = merge_unit // unit_side * 2 + corner // 2
    inner_column = merge_unit % unit_side * 2 + corner % 2
    row_place = window_row[:, :, None] * window_side + inner_row
    column_place = window_column[:, :, None] * window_side + inner_column
    return (row_place, column_place)


def merge_source(height, page_width, slot_row, window_side, position_count):
    position = jnp.arange(position_count, dtype=jnp.int32)
    merge_unit = position // 4
    corner = position % 4
    units_wide = page_width // 2
    unit_row = merge_unit // units_wide
    unit_column = merge_unit % units_wide
    unit_side = window_side // 2
    across = page_width // window_side
    live_rows = unit_row < height // 2
    window = unit_row // unit_side * across + unit_column // unit_side
    window = jnp.where(live_rows, window, 0)
    ordinal = jnp.arange(slot_row.shape[0], dtype=jnp.int32)
    slot_index = jnp.sum(
        jnp.where(window[:, None] == ordinal[None, :], slot_row[None, :], 0), axis=1
    )
    inner = (unit_row % unit_side * unit_side + unit_column % unit_side) * 4 + corner
    inner = jnp.where(live_rows, inner, 0)
    return (slot_index * (window_side * window_side) + inner, live_rows)


def normalize(block_in):
    values = block_in.astype(jnp.float32)
    factor = lax.rsqrt(jnp.mean(values * values, axis=-1, keepdims=True) + EPSILON)
    return (values * factor).astype(jnp.bfloat16)


def settle(array_in):
    return lax.optimization_barrier(array_in.astype(jnp.bfloat16)).astype(jnp.float32)


def attend(projected, cosine_table, sine_table, window_tokens, head_size):
    windows = projected.shape[0] // window_tokens
    head_count = projected.shape[1] // (3 * head_size)
    split_qkv = projected.reshape(windows, window_tokens, head_count, 3, head_size)
    queries = rotate(split_qkv[:, :, :, 0], cosine_table, sine_table).astype(jnp.bfloat16)
    key_block = rotate(split_qkv[:, :, :, 1], cosine_table, sine_table).astype(jnp.bfloat16)
    values = split_qkv[:, :, :, 2].astype(jnp.bfloat16)
    scores = jnp.einsum(
        "wqhd,wkhd->whqk", queries, key_block, preferred_element_type=jnp.float32
    ) / math.sqrt(head_size)
    row_max = jnp.max(scores, axis=-1, keepdims=True)
    lifted = jnp.exp(scores - row_max)
    weights = (lifted / jnp.sum(lifted, axis=-1, keepdims=True)).astype(jnp.bfloat16)
    mixed_heads = jnp.einsum("whqk,wkhd->wqhd", weights, values, preferred_element_type=jnp.float32)
    return mixed_heads.astype(jnp.bfloat16).reshape(windows * window_tokens, head_count * head_size)


def local(patches, w_qkv, w_out, page_rows, page_cols, window_slot):
    seq_index = lax.axis_index("seq")
    seq_count = lax.axis_size("seq")
    mp_index = lax.axis_index("mp")
    page_count = window_slot.shape[0]
    slot_count = window_slot.shape[1]
    slots_held = slot_count // seq_count
    window_tokens = WS * WS
    slot_numbers = seq_index * slots_held + jnp.arange(slots_held, dtype=jnp.int32)
    row_place, column_place = slot_positions(page_cols, window_slot, slot_numbers, WS)
    cosine_all, sine_all = angle_tables(
        row_place.reshape(-1, window_tokens), column_place.reshape(-1, window_tokens), HD
    )
    normed = normalize(patches)
    projected = jnp.dot(
        normed, lax.all_gather(w_qkv, "seq", axis=0, tiled=True), preferred_element_type=jnp.float32
    )
    mixed_heads = attend(projected, cosine_all[:, :, None], sine_all[:, :, None], window_tokens, HD)
    partial_value = jnp.dot(
        mixed_heads,
        lax.all_gather(w_out, "seq", axis=1, tiled=True),
        preferred_element_type=jnp.float32,
    )
    branch = lax.psum_scatter(
        settle(partial_value).astype(jnp.bfloat16), "mp", scatter_dimension=1, tiled=True
    ).astype(jnp.float32)
    share_width = branch.shape[1]
    residual = lax.dynamic_slice_in_dim(patches, mp_index * share_width, share_width, 1).astype(
        jnp.float32
    )
    block_out = (residual + branch).astype(jnp.bfloat16)
    sectioned = block_out.reshape(page_count, slots_held * window_tokens, block_out.shape[1])
    landed = lax.all_to_all(sectioned, "seq", split_axis=0, concat_axis=1, tiled=True)
    own_pages = landed.shape[0]
    first_page = seq_index * own_pages
    heights = lax.dynamic_slice_in_dim(page_rows, first_page, own_pages, 0)
    widths = lax.dynamic_slice_in_dim(page_cols, first_page, own_pages, 0)
    slot_rows = lax.dynamic_slice_in_dim(window_slot, first_page, own_pages, 0)

    def regroup(received, height, page_width, slot_row):
        source, live_rows = merge_source(height, page_width, slot_row, WS, received.shape[0])
        picked = jnp.take(received, source, axis=0)
        return jnp.where(live_rows[:, None], picked, jnp.zeros_like(picked))

    merged = jax.vmap(regroup)(landed, heights, widths, slot_rows)
    return merged.reshape(-1, merged.shape[2])


def solution(mesh):
    return jax.shard_map(
        local,
        mesh=mesh,
        in_specs=(P("seq", None), P("seq", "mp"), P("mp", "seq"), P(), P(), P()),
        out_specs=P("seq", "mp"),
        check_vma=False,
    )
```

profile of v0, /device:TPU:1, one launch (start us, length us, event | category | flops | bytes accessed | tf_op | source)
XLA Modules:
  0.0 510.5 jit_solution(9554010901288428797)
XLA Ops:
  7.3 55.3 %all-gather.1 = bf16[64,20,320]{2,1,0:T(8,128)(2,1)S(1)} all-gather(bf16[1,20,320]{2,1,0:T(8,128)(2,1)} %bitcast.49), channel_id=1, replica_groups=mesh['seq'=64,'mp'=4] {'seq'}, dimensions={0}, use_global_device_ids=true | all-gather | bytes 832000 | tf_op jit(solution)/shard_map/all_gather | solution.py:121
  65.8 6.3 %fusion.1 = f32[4096]{0:T(1024)S(1)} fusion(bf16[4096,1280]{1,0:T(8,128)(2,1)} %param.6), kind=kLoop, calls=%fused_computation.4 | loop fusion | flops 15724544 | bytes 10502144 | tf_op jit(solution)/shard_map/reduce_sum | solution.py:76
  72.4 10.1 %fusion.24 = (f32[64,64,80]{1,0,2:T(8,128)S(1)}, f32[64,64,80]{1,0,2:T(8,128)}) fusion(f32[64,64,20]{1,0,2:T(8,128)S(1)} %get-tuple-element.18, f32[64,64,20]{1,0,2:T(8,128)S(1)} %get-tuple-element.17), kind=kLoop, calls=%fused_computation.36 | loop fusion | flops 983040 | bytes 3276800 | tf_op jit(solution)/shard_map/cos | solution.py:32
  82.5 9.9 %all-gather.4.cloned.1.call-done = bf16[64,20,960]{2,1,0:T(8,128)(2,1)} async-done(((bf16[1,20,960]{2,1,0:T(8,128)(2,1)}), bf16[64,20,960]{2,1,0:T(8,128)(2,1)}) %all-gather.4.cloned.1.call-update) | async-done | bytes 2457616 | tf_op jit(solution)/shard_map/all_gather | solution.py:116
  92.4 5.5 %reshape.727 = bf16[1280,960]{1,0:T(8,128)(2,1)} reshape(bf16[64,20,960]{2,1,0:T(8,128)(2,1)} %all-gather.4.cloned.1.call-done) | data formatting | bytes 4915200
  97.9 17.2 %fusion.3 = f32[4096,960]{0,1:T(8,128)} fusion(bf16[1280,960]{1,0:T(8,128)(2,1)} %reshape.727, bf16[4096,1280]{1,0:T(8,128)(2,1)} %param.6, f32[4096]{0:T(1024)S(1)} %add_rsqrt_fusion), kind=kOutput, calls=%fused_computation.7 | convolution fusion | flops 10082058240 | bytes 28688384 | tf_op jit(solution)/shard_map/dot_general | solution.py:115
  115.2 25.2 %reshape.714 = f32[64,64,4,3,80]{1,0,4,3,2:T(8,128)} reshape(f32[4096,960]{0,1:T(8,128)} %fusion.3) | data formatting | bytes 31457280 | tf_op jit(solution)/shard_map/reshape | solution.py:87
  140.4 13.1 %slice_bitcast_fusion.1 = (f32[64,64,4,80]{1,0,3,2:T(8,128)S(1)}, f32[64,64,4,80]{1,0,3,2:T(8,128)}) fusion(f32[64,64,4,3,80]{1,0,4,3,2:T(8,128)} %reshape.714), kind=kLoop, calls=%fused_computation.9 | loop fusion | bytes 20971520 | tf_op jit(solution)/shard_map/squeeze | solution.py:88
  153.5 7.7 %slice.31 = bf16[64,64,4,1,80]{1,0,4,3,2:T(8,128)(2,1)} slice(f32[64,64,4,3,80]{1,0,4,3,2:T(8,128)} %reshape.714), slice={[0:64], [0:64], [0:4], [2:3], [0:80]} | slice | bytes 5242880 | tf_op jit(solution)/shard_map/slice | solution.py:90
  161.2 10.2 %slice_negate_fusion = (f32[64,64,4,40]{1,0,3,2:T(8,128)}, f32[64,64,4,40]{1,0,3,2:T(8,128)}, f32[64,64,4,40]{1,0,3,2:T(8,128)}, f32[64,64,4,40]{1,0,3,2:T(8,128)}) fusion(f32[64,64,4,80]{1,0,3,2:T(8,128)} %get-tuple-element.10, f32[64,64,4,80]{1,0,3,2:T(8,128)S(1)} %get-tuple-element.9), kind=kLoop, calls=%fused_computation.22 | loop fusion | flops 1310720 | bytes 20971520 | tf_op jit(solution)/shard_map/neg | solution.py:17
  171.5 19.6 %fusion.6 = (bf16[64,64,4,80]{1,0,3,2:T(8,128)(2,1)}, bf16[64,64,4,80]{1,0,3,2:T(8,128)(2,1)}) fusion(f32[64,64,4,40]{1,0,3,2:T(8,128)} %get-tuple-element.21, f32[64,64,4,40]{1,0,3,2:T(8,128)} %get-tuple-element.22, f32[64,64,80]{1,0,2:T(8,128)} %get-tuple-element.16, f32[64,64,80]{1,0,2:T(8,128)S(1)} %get-tuple-element.15, ...), kind=kLoop, calls=%fused_computation.12 | loop fusion | flops 13107200 | bytes 28835840 | tf_op jit(solution)/shard_map/convert_element_type | solution.py:88
  191.0 16.8 %fusion.13 = f32[64,4,64,64]{2,3,1,0:T(8,128)S(1)} fusion(bf16[64,64,4,80]{1,0,3,2:T(8,128)(2,1)} %get-tuple-element.8, bf16[64,64,4,80]{1,0,3,2:T(8,128)(2,1)} %get-tuple-element.7), kind=kOutput, calls=%fused_computation.24 | convolution fusion | flops 167772160 | bytes 9437184 | tf_op jit(solution)/shard_map/wqhd,wkhd->whqk/dot_general | solution.py:91
  212.3 8.2 %copy.37 = bf16[64,64,4,1,80]{4,1,2,0,3:T(8,128)(2,1)} copy(bf16[64,64,4,1,80]{1,0,4,3,2:T(8,128)(2,1)} %slice.31) | data formatting | bytes 5242880
  220.5 6.2 %convert_bitcast_fusion = bf16[64,64,4,80]{3,1,2,0:T(8,128)(2,1)S(1)} fusion(f32[64,4,64,64]{2,3,1,0:T(8,128)} %get-tuple-element.20, f32[64,4,64]{2,1,0:T(4,128)S(1)} %get-tuple-element.19, bf16[64,64,4,1,80]{4,1,2,0,3:T(8,128)(2,1)} %copy.37), kind=kOutput, calls=%fused_computation.29 | convolution fusion | flops 171180032 | bytes 9502720 | tf_op jit(solution)/shard_map/whqk,wkhd->wqhd/dot_general | solution.py:97
  226.8 10.2 %copy.31 = bf16[64,64,4,80]{3,2,1,0:T(4,128)(2,1)} copy(bf16[64,64,4,80]{3,1,2,0:T(8,128)(2,1)S(1)} %convert_bitcast_fusion) | data formatting | bytes 5242880 | tf_op jit(solution)/shard_map/convert_element_type | solution.py:98
  237.0 6.4 %reshape.715 = bf16[4096,320]{1,0:T(8,128)(2,1)S(1)} reshape(bf16[64,64,4,80]{3,2,1,0:T(4,128)(2,1)} %copy.31) | data formatting | bytes 5242880 | tf_op jit(solution)/shard_map/reshape | solution.py:98
  243.4 9.6 %convolution_convert_fusion = bf16[4096,1280]{1,0:T(8,128)(2,1)} fusion(bf16[4096,320]{1,0:T(8,128)(2,1)S(1)} %reshape.715, bf16[1280,320]{1,0:T(8,128)(2,1)} %reshape.729), kind=kOutput, calls=%fused_computation.6 | convolution fusion | flops 3360686080 | bytes 13926400 | tf_op jit(solution)/shard_map/dot_general | solution.py:119
  252.9 14.3 %copy.34 = bf16[4096,1280]{0,1:T(8,128)(2,1)} copy(bf16[4096,1280]{1,0:T(8,128)(2,1)} %convolution_convert_fusion) | data formatting | bytes 20971520
  267.3 97.0 %reduce-scatter.4.cloned.1.call-done = bf16[320,4096]{1,0:T(8,128)(2,1)} async-done(((bf16[1280,4096]{1,0:T(8,128)(2,1)}), bf16[320,4096]{1,0:T(8,128)(2,1)}) %reduce-scatter.4.cloned.1.call-update) | async-done | bytes 2621456
  367.6 5.9 %add_convert_fusion = bf16[4096,320]{1,0:T(8,128)(2,1)} fusion(bf16[4096,320]{1,0:T(8,128)(2,1)S(1)} %copy.35, bf16[4096,1280]{1,0:T(8,128)(2,1)} %param.6, s32[]{:T(128)S(6)} %select_n.400), kind=kLoop, calls=%fused_computation.21 | loop fusion | flops 5242880 | bytes 7864324 | tf_op jit(solution)/shard_map/convert_element_type | solution.py:131
  373.5 11.3 %all-to-all-start = ((bf16[64,64,320]{2,1,0:T(8,128)(2,1)}), bf16[64,64,320]{2,1,0:T(8,128)(2,1)S(1)}, u32[]{:S(2)}, u32[]{:S(2)}) async-start(bf16[64,64,320]{2,1,0:T(8,128)(2,1)} %bitcast.45), calls=%async_computation | async-start | bytes 6291456 | tf_op jit(solution)/shard_map/all_to_all | solution.py:133
  395.7 61.4 %all-to-all-done = bf16[64,64,320]{2,1,0:T(8,128)(2,1)S(1)} async-done(((bf16[64,64,320]{2,1,0:T(8,128)(2,1)}), bf16[64,64,320]{2,1,0:T(8,128)(2,1)S(1)}, u32[]{:S(2)}, u32[]{:S(2)}) %all-to-all-start) | async-done | bytes 2621472 | tf_op jit(solution)/shard_map/all_to_all | solution.py:133
  457.0 38.6 %gather_fusion = bf16[4096,320]{1,0:T(8,128)(2,1)} fusion(bf16[1,4096,320]{2,1,0:T(8,128)(2,1)S(1)} %bitcast.43, s32[4096]{0:T(1024)S(1)} %bitcast.42), kind=kCustom, calls=%fused_computation | custom fusion | bytes 5275648 | tf_op jit(solution)/shard_map/vmap(jit(_take))/gather | solution.py:142
  495.6 5.0 select_select_fusion
  (31 shorter events, 20.4 us)
Async XLA Ops:
  6.5 85.9 %all-gather.4.cloned.1.call-start = ((), (), s32[]{:S(2)}) async-start(), calls=%async_computation.2 | async-start | bytes 3194880 | tf_op jit(solution)/shard_map/all_gather | solution.py:116
  7.3 357.0 %reduce-scatter.4.cloned.1.call-start = ((), (), s32[]{:S(2)}) async-start(), calls=%async_computation.3 | async-start | bytes 13107200
  373.5 11.3 %copy-start = (s32[64]{0:T(128)S(1)}, s32[64]{0:T(128)}, u32[]{:S(2)}) copy-start(s32[64]{0:T(128)} %param.10) | copy-start | bytes 772
  373.5 14.5 %copy-start.1 = (s32[64]{0:T(128)S(1)}, s32[64]{0:T(128)}, u32[]{:S(2)}) copy-start(s32[64]{0:T(128)} %param.9) | copy-start | bytes 772
  373.5 83.6 %all-to-all-start = ((bf16[64,64,320]{2,1,0:T(8,128)(2,1)}), bf16[64,64,320]{2,1,0:T(8,128)(2,1)S(1)}, u32[]{:S(2)}, u32[]{:S(2)}) async-start(bf16[64,64,320]{2,1,0:T(8,128)(2,1)} %bitcast.45), calls=%async_computation | async-start | bytes 6291456 | tf_op jit(solution)/shard_map/all_to_all | solution.py:133
Sparse Core Ops, SparseCore 0:
  10.1 82.3 all-gather.3
  267.4 96.8 reduce-scatter.3
where the time goes:
time: 515 us; the launch traced here: 510 us
  waiting for transfers between devices  169 us (33%)
  local copies, waits for them, and re-layouts  138 us (27%)
  other arithmetic  67.4 us (13%)
  blocking collectives  55.3 us (11%)
  matrix products  49.8 us (10%)
  between operations  19.1 us (4%)
  starting transfers between devices  11.3 us (2%)
    unnamed x3, waiting for transfers between devices  97.8 us
    all_to_all x1, waiting for transfers between devices, local(): lax.all_to_all(sectioned, 'seq', split_axis=0, concat_axis=1, tiled=True)  61.4 us
    all_gather x1, blocking collectives, local(): lax.all_gather(w_out, 'seq', axis=1, tiled=True)  55.3 us
    gather x2, local copies, waits for them, and re-layouts, regroup(): picked = jnp.take(received, source, axis=0)  38.6 us
    unnamed x9, local copies, waits for them, and re-layouts  32.7 us
    reshape x1, local copies, waits for them, and re-layouts, attend(): projected.reshape(windows, window_tokens, head_count, 3, head_size)  25.2 us
    convert_element_type x1, other arithmetic, attend(): rotate(split_qkv[:, :, :, 0], cosine_table, sine_table).astype(jnp.bfloat16)  19.6 us
    dot_general x1, matrix products, local(): jnp.dot(normed, lax.all_gather(w_qkv, 'seq', axis=0, tiled=True), preferr...  17.2 us
  transfers between devices with their start and end apart: 3, of which 3 were waited for; matrix products, arithmetic and copies ran while one was open for 5% of the time, Pallas kernels for 0%

commit v1 on v0

v1 whole, which is shorter than its diff:
```python
import jax
import jax.numpy as jnp
from jax import lax
from jax.sharding import PartitionSpec as P

HD = 80
WS = 8
QUARTERS = 4


EPSILON = 1e-06


def angle_tables(row_place, column_place, head_size):
    quarter = head_size // 4
    frequency = 1.0 / 10000.0 ** (jnp.arange(quarter, dtype=jnp.float32) * 2.0 / (head_size // 2))
    angles = jnp.concatenate(
        [
            row_place[..., None].astype(jnp.float32) * frequency,
            column_place[..., None].astype(jnp.float32) * frequency,
        ],
        axis=-1,
    )
    angles = jnp.concatenate([angles, angles], axis=-1)
    return (jnp.cos(angles), jnp.sin(angles))


def slot_positions(page_widths, slot_table, slot_numbers, window_side):
    matches = slot_table[:, :, None] == slot_numbers[None, None, :]
    ordinal = jnp.arange(slot_table.shape[1], dtype=jnp.int32)
    window = jnp.sum(jnp.where(matches, ordinal[None, :, None], 0), axis=1)
    across = page_widths // window_side
    window_row = window // across[:, None]
    window_column = window % across[:, None]
    unit_side = window_side // 2
    position = jnp.arange(window_side * window_side, dtype=jnp.int32)
    merge_unit = position // 4
    corner = position % 4
    inner_row = merge_unit // unit_side * 2 + corner // 2
    inner_column = merge_unit % unit_side * 2 + corner % 2
    row_place = window_row[:, :, None] * window_side + inner_row
    column_place = window_column[:, :, None] * window_side + inner_column
    return (row_place, column_place)


def block_sources(height, page_width, slot_row, block_count):
    across = page_width // WS
    block = jnp.arange(block_count, dtype=jnp.int32)
    band = block // across
    column = block % across
    window_row = band // QUARTERS
    quarter = band % QUARTERS
    live = window_row < height // WS
    window = jnp.where(live, window_row * across + column, 0)
    ordinal = jnp.arange(slot_row.shape[0], dtype=jnp.int32)
    slot = jnp.sum(jnp.where(window[:, None] == ordinal[None, :], slot_row[None, :], 0), axis=1)
    return (slot * QUARTERS + quarter, live)


def normalize(block_in):
    values = block_in.astype(jnp.float32)
    factor = lax.rsqrt(jnp.mean(values * values, axis=-1, keepdims=True) + EPSILON)
    return (values * factor).astype(jnp.bfloat16)


def rotated_columns(weight):
    half = weight.shape[-1] // 2
    return jnp.concatenate([-weight[..., half:], weight[..., :half]], axis=-1)


def local(patches, w_qkv, w_out, page_rows, page_cols, window_slot):
    seq_index = lax.axis_index("seq")
    seq_count = lax.axis_size("seq")
    mp_index = lax.axis_index("mp")
    page_count = window_slot.shape[0]
    slot_count = window_slot.shape[1]
    slots_held = slot_count // seq_count
    window_tokens = WS * WS
    quarter_tokens = window_tokens // QUARTERS
    model_width = patches.shape[1]
    windows = patches.shape[0] // window_tokens

    joined = lax.all_gather(
        jnp.concatenate([w_qkv, w_out.T], axis=1), "seq", axis=0, tiled=True
    )
    qkv = joined[:, : w_qkv.shape[1]]
    out_rows_t = joined[:, w_qkv.shape[1] :]
    heads = qkv.shape[1] // (3 * HD)
    qkv = qkv.reshape(model_width, heads, 3, HD)
    w_q = qkv[:, :, 0]
    w_k = qkv[:, :, 1]
    w_v = qkv[:, :, 2].reshape(model_width, heads * HD)
    fused = jnp.concatenate(
        [
            w_q.reshape(model_width, heads * HD),
            w_k.reshape(model_width, heads * HD),
            rotated_columns(w_q).reshape(model_width, heads * HD),
            rotated_columns(w_k).reshape(model_width, heads * HD),
            w_v,
        ],
        axis=1,
    )
    out_full_t = lax.all_gather(out_rows_t, "mp", axis=1, tiled=True)

    slot_numbers = seq_index * slots_held + jnp.arange(slots_held, dtype=jnp.int32)
    row_place, column_place = slot_positions(page_cols, window_slot, slot_numbers, WS)
    cosine, sine = angle_tables(
        row_place.reshape(-1, window_tokens), column_place.reshape(-1, window_tokens), HD
    )
    cosine = jnp.tile(cosine.reshape(-1, HD), (1, 2 * heads))
    sine = jnp.tile(sine.reshape(-1, HD), (1, 2 * heads))

    normed = normalize(patches)
    projected = jnp.dot(normed, fused, preferred_element_type=jnp.float32)
    width = heads * HD
    turned = projected[:, : 2 * width] * cosine + projected[:, 2 * width : 4 * width] * sine
    turned = turned.astype(jnp.bfloat16).reshape(windows, window_tokens, 2 * width)
    queries = turned[:, :, :width]
    key_block = turned[:, :, width:]
    values = projected[:, 4 * width :].astype(jnp.bfloat16).reshape(windows, window_tokens, width)

    lane_head = jnp.arange(width, dtype=jnp.int32) // HD
    scale = 1.0 / (HD ** 0.5)
    mixed = jnp.zeros((windows, window_tokens, width), jnp.float32)
    for head in range(heads):
        mask = lane_head == head
        picked = jnp.where(mask, queries, jnp.zeros_like(queries))
        scores = jnp.einsum(
            "wqd,wkd->wqk", picked, key_block, preferred_element_type=jnp.float32
        ) * scale
        row_max = jnp.max(scores, axis=-1, keepdims=True)
        lifted = jnp.exp(scores - row_max)
        weights = (lifted / jnp.sum(lifted, axis=-1, keepdims=True)).astype(jnp.bfloat16)
        own_values = jnp.where(mask, values, jnp.zeros_like(values))
        mixed = mixed + jnp.einsum(
            "wqk,wkd->wqd", weights, own_values, preferred_element_type=jnp.float32
        )
    mixed = mixed.astype(jnp.bfloat16)

    spread = mixed.reshape(windows, QUARTERS, quarter_tokens, 1, width)
    gathered = lax.all_to_all(spread, "mp", split_axis=1, concat_axis=3, tiled=True)
    gathered = gathered.reshape(windows * quarter_tokens, QUARTERS * width)

    branch = lax.dot_general(
        gathered, out_full_t, (((1,), (1,)), ((), ())), preferred_element_type=jnp.float32
    )
    residual = patches.reshape(windows, QUARTERS, quarter_tokens, model_width)
    residual = lax.dynamic_index_in_dim(residual, mp_index, 1, keepdims=False)
    residual = residual.reshape(windows * quarter_tokens, model_width).astype(jnp.float32)
    block_out = (residual + branch).astype(jnp.bfloat16)

    share_width = model_width // QUARTERS
    sectioned = block_out.reshape(page_count, quarter_tokens, QUARTERS, share_width)
    sectioned = jnp.transpose(sectioned, (0, 2, 1, 3)).reshape(
        page_count * QUARTERS, quarter_tokens, share_width
    )
    landed = lax.all_to_all(sectioned, ("seq", "mp"), split_axis=0, concat_axis=0, tiled=True)

    own_pages = page_count // seq_count
    first_page = seq_index * own_pages
    heights = lax.dynamic_slice_in_dim(page_rows, first_page, own_pages, 0)
    widths = lax.dynamic_slice_in_dim(page_cols, first_page, own_pages, 0)
    slot_rows = lax.dynamic_slice_in_dim(window_slot, first_page, own_pages, 0)
    block_count = slot_count * QUARTERS // own_pages

    landed = landed.reshape(own_pages, block_count, quarter_tokens, share_width)

    def regroup(received, height, page_width, slot_row):
        source, live = block_sources(height, page_width, slot_row, block_count)
        picked = jnp.take(received, source, axis=0)
        return jnp.where(live[:, None, None], picked, jnp.zeros_like(picked))

    merged = jax.vmap(regroup)(landed, heights, widths, slot_rows)
    return merged.reshape(-1, share_width)


def solution(mesh):
    return jax.shard_map(
        local,
        mesh=mesh,
        in_specs=(P("seq", None), P("seq", "mp"), P("mp", "seq"), P(), P(), P()),
        out_specs=P("seq", "mp"),
        check_vma=False,
    )
```

time: 515 us -> 383 us (0.74)
  local copies, waits for them, and re-layouts: 138 us -> 66.5 us
  blocking collectives: 55.3 us -> 0 us
  other arithmetic: 67.4 us -> 32.3 us
  matrix products: 49.8 us -> 73.8 us
    unnamed x3 -> x2, waiting for transfers between devices: 97.8 us -> 0.03 us
    all_gather x1 -> x2, waiting for transfers between devices: 9.95 us -> 70.3 us  [the longest x1 70.3 us: local(): lax.all_gather(jnp.concatenate([w_qkv, w_out.T], axis=1), 'seq', axis=0,...]
    all_gather x1 -> x0, blocking collectives: 55.3 us -> none  [local(): lax.all_gather(w_out, 'seq', axis=1, tiled=True)]
    all_to_all x1 -> x2, waiting for transfers between devices: 61.4 us -> 102 us  [the longest x1 67.9 us: local(): lax.all_to_all(sectioned, ('seq', 'mp'), split_axis=0, concat_axis=0, til...]
    gather x2, local copies, waits for them, and re-layouts: 38.6 us -> 2.73 us  [regroup(): picked = jnp.take(received, source, axis=0)]
    dot_general x4 -> x10, matrix products: 49.8 us -> 73.8 us  [the longest x4 26.1 us: local(): jnp.einsum('wqk,wkd->wqd', weights, own_values, preferred_element_type=jn...]
    unnamed x9 -> x23, local copies, waits for them, and re-layouts: 32.7 us -> 10.6 us
    convert_element_type x2 -> x1, other arithmetic: 25.4 us -> 4.69 us  [local(): turned.astype(jnp.bfloat16).reshape(windows, window_tokens, 2 * width)]
  transfers between devices with their start and end apart: 3 -> 4, of which waited for: 3 -> 3; matrix products, arithmetic and copies ran while one was open for 5% -> 17% of each run, Pallas kernels for 0% -> 0%
where the time goes in v1:
time: 383 us; the launch traced here: 379 us
  waiting for transfers between devices  172 us (45%)
  matrix products  73.8 us (19%)
  local copies, waits for them, and re-layouts  66.5 us (17%)
  other arithmetic  32.3 us (8%)
  between operations  19.3 us (5%)
  starting transfers between devices  15.1 us (4%)
    all_gather x1, waiting for transfers between devices, local(): lax.all_gather(jnp.concatenate([w_qkv, w_out.T], axis=1), 'seq', axis=0,...  70.3 us
    all_to_all x1, waiting for transfers between devices, local(): lax.all_to_all(sectioned, ('seq', 'mp'), split_axis=0, concat_axis=0, til...  67.9 us
    all_to_all x1, waiting for transfers between devices, local(): lax.all_to_all(spread, 'mp', split_axis=1, concat_axis=3, tiled=True)  33.7 us
    dot_general x4, matrix products, local(): jnp.einsum('wqk,wkd->wqd', weights, own_values, preferred_element_type=jn...  26.1 us
    dot_general x1, matrix products, local(): projected = jnp.dot(normed, fused, preferred_element_type=jnp.float32)  21.3 us
    dot_general x4, matrix products, local(): jnp.einsum('wqd,wkd->wqk', picked, key_block, preferred_element_type=jnp....  19.2 us
    all_to_all x1, starting transfers between devices, local(): lax.all_to_all(sectioned, ('seq', 'mp'), split_axis=0, concat_axis=0, til...  10.8 us
    unnamed x23, local copies, waits for them, and re-layouts  10.6 us
  transfers between devices with their start and end apart: 4, of which 3 were waited for; matrix products, arithmetic and copies ran while one was open for 17% of the time, Pallas kernels for 0%

profile of v1, /device:TPU:1, one launch (start us, length us, event | category | flops | bytes accessed | tf_op | source)
XLA Modules:
  0.0 378.8 jit_solution(3544385893247369594)
XLA Ops:
  10.3 6.1 %fusion.4 = f32[4096]{0:T(1024)S(1)} fusion(bf16[4096,1280]{1,0:T(8,128)(2,1)} %param.6), kind=kLoop, calls=%fused_computation.7 | loop fusion | flops 15724544 | bytes 10502144 | tf_op jit(solution)/shard_map/reduce_sum | solution.py:62
  16.6 6.2 %fusion.68 = (f32[4096,80]{0,1:T(8,128)}, f32[4096,80]{0,1:T(8,128)}) fusion(f32[4096,20]{0,1:T(8,128)S(1)} %get-tuple-element.19, f32[4096,20]{0,1:T(8,128)S(1)} %get-tuple-element.18), kind=kLoop, calls=%fused_computation.87 | loop fusion | flops 983040 | bytes 3276800 | tf_op jit(solution)/shard_map/cos | solution.py:25
  22.8 70.3 %all-gather.6.cloned.1.call-done = bf16[64,20,1280]{2,1,0:T(8,128)(2,1)} async-done(((bf16[1,20,1280]{2,1,0:T(8,128)(2,1)}), bf16[64,20,1280]{2,1,0:T(8,128)(2,1)}) %all-gather.6.cloned.1.call-update) | async-done | bytes 3276816 | tf_op jit(solution)/shard_map/all_gather | solution.py:83
  93.1 4.6 %reshape.661 = bf16[1280,1280]{1,0:T(8,128)(2,1)S(1)} reshape(bf16[64,20,1280]{2,1,0:T(8,128)(2,1)} %all-gather.6.cloned.1.call-done) | data formatting | bytes 6553600
  109.5 21.3 %fusion.6 = f32[4096,1600]{0,1:T(8,128)S(1)} fusion(bf16[1280,1600]{0,1:T(8,128)(2,1)} %constant_dynamic-update-slice_fusion, bf16[4096,1280]{1,0:T(8,128)(2,1)} %param.6, f32[4096]{0:T(1024)S(1)} %add_rsqrt_fusion), kind=kOutput, calls=%fused_computation.9 | convolution fusion | flops 16792944640 | bytes 40812544 | tf_op jit(solution)/shard_map/dot_general | solution.py:114
  133.5 4.7 %fusion.9 = bf16[4096,640]{0,1:T(8,128)(2,1)} fusion(f32[4096,1600]{0,1:T(8,128)S(1)} %fusion.6, f32[4096,80]{0,1:T(8,128)S(1)} %copy-done.2, f32[4096,80]{0,1:T(8,128)S(1)} %copy-done.1), kind=kLoop, calls=%fused_computation.12 | loop fusion | flops 10485760 | bytes 28835840 | tf_op jit(solution)/shard_map/convert_element_type | solution.py:117
  138.2 7.9 %copy.44 = bf16[4096,640]{1,0:T(8,128)(2,1)} copy(bf16[4096,640]{0,1:T(8,128)(2,1)} %fusion.9) | data formatting | bytes 10485760 | tf_op jit(solution)/shard_map/convert_element_type | solution.py:117
  146.0 4.2 %fusion.23 = f32[64,64,64]{1,2,0:T(8,128)S(1)} fusion(pred[320]{0:T(512)(128)(4,1)S(1)} %broadcast_compare_fusion.3, bf16[64,64,640]{2,1,0:T(8,128)(2,1)} %bitcast.63), kind=kOutput, calls=%fused_computation.31 | convolution fusion | flops 169082880 | bytes 7340352 | tf_op jit(solution)/shard_map/wqd,wkd->wqk/dot_general | solution.py:128
  152.2 3.5 copy.45
  155.8 6.7 %fusion.19 = f32[64,64,64]{1,2,0:T(8,128)} fusion(pred[320]{0:T(512)(128)(4,1)S(1)} %broadcast_compare_fusion.1, bf16[64,64,640]{2,1,0:T(8,128)(2,1)} %bitcast.64), kind=kOutput, calls=%fused_computation.27 | convolution fusion | flops 169082880 | bytes 7340352 | tf_op jit(solution)/shard_map/wqd,wkd->wqk/dot_general | solution.py:128
  162.5 5.6 %fusion.15 = f32[64,64,64]{1,2,0:T(8,128)} fusion(pred[320]{0:T(512)(128)(4,1)S(1)} %broadcast_compare_fusion, bf16[64,64,640]{2,1,0:T(8,128)(2,1)} %bitcast.65), kind=kOutput, calls=%fused_computation.23 | convolution fusion | flops 169082880 | bytes 7340352 | tf_op jit(solution)/shard_map/wqd,wkd->wqk/dot_general | solution.py:128
  178.4 5.4 %fusion.21 = f32[64,64,320]{2,1,0:T(8,128)} fusion(bf16[64,64,320]{2,1,0:T(8,128)(2,1)S(1)} %bitcast.58, pred[320]{0:T(512)(128)(4,1)S(1)} %broadcast_compare_fusion.3, f32[64,64]{1,0:T(8,128)S(1)} %fusion.127, f32[64,64,64]{1,2,0:T(8,128)} %copy-done.6), kind=kOutput, calls=%fused_computation.29 | convolution fusion | flops 170135616 | bytes 8929600 | tf_op jit(solution)/shard_map/wqk,wkd->wqd/dot_general | solution.py:135
  183.8 5.5 %fusion.17 = f32[64,64,320]{2,1,0:T(8,128)} fusion(bf16[64,64,320]{2,1,0:T(8,128)(2,1)S(1)} %bitcast.59, pred[320]{0:T(512)(128)(4,1)S(1)} %broadcast_compare_fusion.1, f32[64,64]{1,0:T(8,128)S(1)} %fusion.126, f32[64,64,64]{1,2,0:T(8,128)} %fusion.19), kind=kOutput, calls=%fused_computation.25 | convolution fusion | flops 170135616 | bytes 8929600 | tf_op jit(solution)/shard_map/wqk,wkd->wqd/dot_general | solution.py:135
  189.3 5.4 %fusion.13 = f32[64,64,320]{2,1,0:T(8,128)} fusion(bf16[64,64,320]{2,1,0:T(8,128)(2,1)S(1)} %bitcast.60, pred[320]{0:T(512)(128)(4,1)S(1)} %broadcast_compare_fusion, f32[64,64]{1,0:T(8,128)S(1)} %fusion.125, f32[64,64,64]{1,2,0:T(8,128)} %fusion.15), kind=kOutput, calls=%fused_computation.21 | convolution fusion | flops 170135616 | bytes 8929600 | tf_op jit(solution)/shard_map/wqk,wkd->wqd/dot_general | solution.py:135
  194.7 9.9 %add_convert_fusion = bf16[64,64,320]{2,1,0:T(8,128)(2,1)S(1)} fusion(f32[64,64,320]{2,1,0:T(8,128)} %fusion.13, f32[64,64,320]{2,1,0:T(8,128)} %fusion.17, f32[64,64,320]{2,1,0:T(8,128)} %fusion.21, bf16[64,64,320]{2,1,0:T(8,128)(2,1)} %bitcast.61, pred[320]{0:T(512)(128)(4,1)S(1)} %broadcast_compare_fusion.2, f32[64,64]{1,0:T(8,128)S(1)} %fusion.128, ...), kind=kOutput, calls=%fused_computation.15 | convolution fusion | flops 175378496 | bytes 22036800 | tf_op jit(solution)/shard_map/wqk,wkd->wqd/dot_general | solution.py:135
  206.5 4.2 %all-to-all-start = ((bf16[64,4,16,1,320]{4,2,0,3,1:T(8,128)(2,1)}), bf16[64,4,16,1,320]{4,2,0,3,1:T(8,128)(2,1)S(1)}, u32[]{:S(2)}, u32[]{:S(2)}) async-start(bf16[64,4,16,1,320]{4,2,0,3,1:T(8,128)(2,1)} %copy.50), calls=%async_computation | async-start | bytes 6291456 | tf_op jit(solution)/shard_map/all_to_all | solution.py:141
  214.2 33.7 %all-to-all-done = bf16[64,4,16,1,320]{4,2,0,3,1:T(8,128)(2,1)S(1)} async-done(((bf16[64,4,16,1,320]{4,2,0,3,1:T(8,128)(2,1)}), bf16[64,4,16,1,320]{4,2,0,3,1:T(8,128)(2,1)S(1)}, u32[]{:S(2)}, u32[]{:S(2)}) %all-to-all-start) | async-done | bytes 2621472 | tf_op jit(solution)/shard_map/all_to_all | solution.py:141
  247.8 5.7 %copy.51 = bf16[64,1,16,4,1,320]{5,3,2,0,4,1:T(4,128)(2,1)} copy(bf16[64,1,16,4,1,320]{5,2,0,3,4,1:T(8,128)(2,1)S(1)} %bitcast.56) | data formatting | bytes 5242880 | tf_op jit(solution)/shard_map/all_to_all | solution.py:141
  253.6 5.1 %reshape.646 = bf16[1024,1280]{1,0:T(8,128)(2,1)S(1)} reshape(bf16[64,1,16,4,1,320]{5,3,2,0,4,1:T(4,128)(2,1)} %copy.51) | data formatting | bytes 5242880 | tf_op jit(solution)/shard_map/reshape | solution.py:142
  258.7 7.1 %fusion.11 = bf16[1024,1280]{1,0:T(8,128)(2,1)} fusion(bf16[1024,1280]{1,0:T(8,128)(2,1)} %bitcast.74, bf16[1024,1280]{1,0:T(8,128)(2,1)S(1)} %reshape.646, bf16[1280,1280]{0,1:T(8,128)(2,1)} %all-gather.4.cloned.1.call-done), kind=kOutput, calls=%fused_computation.18 | convolution fusion | flops 3359375360 | bytes 11141120 | tf_op jit(solution)/shard_map/dot_general | solution.py:144
  265.9 6.1 %reshape.647 = bf16[64,16,4,320]{3,2,1,0:T(4,128)(2,1)S(1)} reshape(bf16[1024,1280]{1,0:T(8,128)(2,1)} %fusion.11) | data formatting | bytes 5242880 | tf_op jit(solution)/shard_map/reshape | solution.py:153
  274.4 10.8 %all-to-all-start.1 = ((bf16[256,16,320]{2,1,0:T(8,128)(2,1)}), bf16[256,16,320]{2,1,0:T(8,128)(2,1)S(1)}, u32[]{:S(2)}, u32[]{:S(2)}) async-start(bf16[256,16,320]{2,1,0:T(8,128)(2,1)} %bitcast.55), calls=%async_computation.1 | async-start | bytes 6291456 | tf_op jit(solution)/shard_map/all_to_all | solution.py:157
  293.2 67.9 %all-to-all-done.1 = bf16[256,16,320]{2,1,0:T(8,128)(2,1)S(1)} async-done(((bf16[256,16,320]{2,1,0:T(8,128)(2,1)}), bf16[256,16,320]{2,1,0:T(8,128)(2,1)S(1)}, u32[]{:S(2)}, u32[]{:S(2)}) %all-to-all-start.1) | async-done | bytes 2621472 | tf_op jit(solution)/shard_map/all_to_all | solution.py:157
  363.8 5.0 %fusion.12 = bf16[4096,320]{1,0:T(8,128)(2,1)S(1)} fusion(bf16[256,16,320]{2,1,0:T(8,128)(2,1)} %gather_fusion, pred[4096]{0:T(1024)(128)(4,1)S(1)} %broadcast_in_dim.141, pred[4096]{0:T(1024)(128)(4,1)S(1)} %broadcast_in_dim.135), kind=kLoop, calls=%fused_computation.20 | loop fusion | flops 2621440 | bytes 5251072 | tf_op jit(solution)/shard_map/vmap(jit(_where))/select_n | solution.py:171
  (78 shorter events, 46.6 us)
Async XLA Ops:
  6.5 86.5 %all-gather.6.cloned.1.call-start = ((), (), s32[]{:S(2)}) async-start(), calls=%async_computation.3 | async-start | bytes 3993600 | tf_op jit(solution)/shard_map/all_gather | solution.py:83
  8.1 250.6 %all-gather.4.cloned.1.call-start = ((), (), s32[]{:S(2)}) async-start(), calls=%async_computation.2 | async-start | bytes 4096000 | tf_op jit(solution)/shard_map/all_gather | solution.py:103
  130.8 1.9 copy-start.1
  130.8 2.6 copy-start.2
  150.3 1.3 copy-start.6
  155.8 33.5 %copy-start = (bf16[4096,320]{1,0:T(8,128)(2,1)}, bf16[4096,320]{1,0:T(8,128)(2,1)S(1)}, u32[]{:S(2)}) copy-start(bf16[4096,320]{1,0:T(8,128)(2,1)S(1)} %copy.45) | copy-start | bytes 7864324
  155.8 12.3 %slice-start = ((s8[5242880]{0:T(1024)(128)(4,1)}), s8[4194304]{0:T(1024)(128)(4,1)S(1)}, s32[]{:S(2)}) async-start(s8[5242880]{0:T(1024)(128)(4,1)} %bitcast.66), calls=%async_computation.4 | async-start | bytes 8388608
  162.5 5.6 %slice-start.1 = ((s8[5242880]{0:T(1024)(128)(4,1)}), s8[1048576]{0:T(1024)(128)(4,1)S(1)}, s32[]{:S(2)}) async-start(s8[5242880]{0:T(1024)(128)(4,1)} %bitcast.66), calls=%async_computation.5 | async-start | bytes 2097152
  173.1 4.6 %copy-start.3 = (f32[64,64,64]{1,2,0:T(8,128)S(1)}, f32[64,64,64]{1,2,0:T(8,128)}, u32[]{:S(2)}) copy-start(f32[64,64,64]{1,2,0:T(8,128)} %fusion.27) | copy-start | bytes 3145732
  206.5 41.3 %all-to-all-start = ((bf16[64,4,16,1,320]{4,2,0,3,1:T(8,128)(2,1)}), bf16[64,4,16,1,320]{4,2,0,3,1:T(8,128)(2,1)S(1)}, u32[]{:S(2)}, u32[]{:S(2)}) async-start(bf16[64,4,16,1,320]{4,2,0,3,1:T(8,128)(2,1)} %copy.50), calls=%async_computation | async-start | bytes 6291456 | tf_op jit(solution)/shard_map/all_to_all | solution.py:141
  274.4 10.8 %copy-start.4 = (s32[64]{0:T(128)S(1)}, s32[64]{0:T(128)}, u32[]{:S(2)}) copy-start(s32[64]{0:T(128)} %param.10) | copy-start | bytes 772
  274.4 14.0 %copy-start.5 = (s32[64]{0:T(128)S(1)}, s32[64]{0:T(128)}, u32[]{:S(2)}) copy-start(s32[64]{0:T(128)} %param.9) | copy-start | bytes 772
  274.4 86.7 %all-to-all-start.1 = ((bf16[256,16,320]{2,1,0:T(8,128)(2,1)}), bf16[256,16,320]{2,1,0:T(8,128)(2,1)S(1)}, u32[]{:S(2)}, u32[]{:S(2)}) async-start(bf16[256,16,320]{2,1,0:T(8,128)(2,1)} %bitcast.55), calls=%async_computation.1 | async-start | bytes 6291456 | tf_op jit(solution)/shard_map/all_to_all | solution.py:157
Sparse Core Ops, SparseCore 0:
  10.0 83.0 all-gather.5
  173.2 39.7 all-gather.3

commit v2 on v1

--- a/solution.py
+++ b/solution.py
@@ -6,6 +6,8 @@
 HD = 80
 WS = 8
 QUARTERS = 4
+HALVES = 2
+SEQ_PARTS = ("z", "y", "core")
 
 
 EPSILON = 1e-06
@@ -69,8 +71,8 @@
 
 
 def local(patches, w_qkv, w_out, page_rows, page_cols, window_slot):
-    seq_index = lax.axis_index("seq")
-    seq_count = lax.axis_size("seq")
+    seq_index = lax.axis_index(SEQ_PARTS)
+    seq_count = lax.axis_size(SEQ_PARTS)
     mp_index = lax.axis_index("mp")
     page_count = window_slot.shape[0]
     slot_count = window_slot.shape[1]
@@ -80,9 +82,13 @@
     model_width = patches.shape[1]
     windows = patches.shape[0] // window_tokens
 
-    joined = lax.all_gather(
-        jnp.concatenate([w_qkv, w_out.T], axis=1), "seq", axis=0, tiled=True
-    )
+    joined = jnp.concatenate([w_qkv, w_out.T], axis=1)
+    for name in SEQ_PARTS:
+        joined = lax.all_gather(joined, name, axis=0)
+    part_sizes = [lax.axis_size(name) for name in SEQ_PARTS]
+    joined = joined.reshape(*reversed(part_sizes), *joined.shape[-2:])
+    joined = jnp.transpose(joined, (*reversed(range(len(SEQ_PARTS))), len(SEQ_PARTS), len(SEQ_PARTS) + 1))
+    joined = joined.reshape(-1, joined.shape[-1])
     qkv = joined[:, : w_qkv.shape[1]]
     out_rows_t = joined[:, w_qkv.shape[1] :]
     heads = qkv.shape[1] // (3 * HD)
@@ -121,40 +127,48 @@
 
     lane_head = jnp.arange(width, dtype=jnp.int32) // HD
     scale = 1.0 / (HD ** 0.5)
-    mixed = jnp.zeros((windows, window_tokens, width), jnp.float32)
-    for head in range(heads):
-        mask = lane_head == head
-        picked = jnp.where(mask, queries, jnp.zeros_like(queries))
-        scores = jnp.einsum(
-            "wqd,wkd->wqk", picked, key_block, preferred_element_type=jnp.float32
-        ) * scale
-        row_max = jnp.max(scores, axis=-1, keepdims=True)
-        lifted = jnp.exp(scores - row_max)
-        weights = (lifted / jnp.sum(lifted, axis=-1, keepdims=True)).astype(jnp.bfloat16)
-        own_values = jnp.where(mask, values, jnp.zeros_like(values))
-        mixed = mixed + jnp.einsum(
-            "wqk,wkd->wqd", weights, own_values, preferred_element_type=jnp.float32
+    share_width = model_width // QUARTERS
+    half_tokens = quarter_tokens // HALVES
+    split_queries = queries.reshape(windows, QUARTERS, HALVES, half_tokens, width)
+    residual_all = patches.reshape(windows, QUARTERS, HALVES, half_tokens, model_width)
+    residual_all = lax.dynamic_index_in_dim(residual_all, mp_index, 1, keepdims=False)
+    landed_halves = []
+    for half in range(HALVES):
+        own_queries = split_queries[:, :, half].reshape(windows, QUARTERS * half_tokens, width)
+        mixed = jnp.zeros((windows, QUARTERS * half_tokens, width), jnp.float32)
+        for head in range(heads):
+            mask = lane_head == head
+            picked = jnp.where(mask, own_queries, jnp.zeros_like(own_queries))
+            scores = jnp.einsum(
+                "wqd,wkd->wqk", picked, key_block, preferred_element_type=jnp.float32
+            ) * scale
+            row_max = jnp.max(scores, axis=-1, keepdims=True)
+            lifted = jnp.exp(scores - row_max)
+            weights = (lifted / jnp.sum(lifted, axis=-1, keepdims=True)).astype(jnp.bfloat16)
+            own_values = jnp.where(mask, values, jnp.zeros_like(values))
+            mixed = mixed + jnp.einsum(
+                "wqk,wkd->wqd", weights, own_values, preferred_element_type=jnp.float32
+            )
+        mixed = mixed.astype(jnp.bfloat16)
+
+        spread = mixed.reshape(windows, QUARTERS, half_tokens, 1, width)
+        gathered = lax.all_to_all(spread, "mp", split_axis=1, concat_axis=3, tiled=True)
+        gathered = gathered.reshape(windows * half_tokens, QUARTERS * width)
+
+        branch = lax.dot_general(
+            gathered, out_full_t, (((1,), (1,)), ((), ())), preferred_element_type=jnp.float32
         )
-    mixed = mixed.astype(jnp.bfloat16)
-
-    spread = mixed.reshape(windows, QUARTERS, quarter_tokens, 1, width)
-    gathered = lax.all_to_all(spread, "mp", split_axis=1, concat_axis=3, tiled=True)
-    gathered = gathered.reshape(windows * quarter_tokens, QUARTERS * width)
-
-    branch = lax.dot_general(
-        gathered, out_full_t, (((1,), (1,)), ((), ())), preferred_element_type=jnp.float32
-    )
-    residual = patches.reshape(windows, QUARTERS, quarter_tokens, model_width)
-    residual = lax.dynamic_index_in_dim(residual, mp_index, 1, keepdims=False)
-    residual = residual.reshape(windows * quarter_tokens, model_width).astype(jnp.float32)
-    block_out = (residual + branch).astype(jnp.bfloat16)
-
-    share_width = model_width // QUARTERS
-    sectioned = block_out.reshape(page_count, quarter_tokens, QUARTERS, share_width)
-    sectioned = jnp.transpose(sectioned, (0, 2, 1, 3)).reshape(
-        page_count * QUARTERS, quarter_tokens, share_width
-    )
-    landed = lax.all_to_all(sectioned, ("seq", "mp"), split_axis=0, concat_axis=0, tiled=True)
+        residual = residual_all[:, half].reshape(windows * half_tokens, model_width)
+        block_out = (residual.astype(jnp.float32) + branch).astype(jnp.bfloat16)
+
+        sectioned = block_out.reshape(page_count, half_tokens, QUARTERS, share_width)
+        sectioned = jnp.transpose(sectioned, (0, 2, 1, 3)).reshape(
+            page_count * QUARTERS, half_tokens, share_width
+        )
+        landed_halves.append(
+            lax.all_to_all(sectioned, (*SEQ_PARTS, "mp"), split_axis=0, concat_axis=0, tiled=True)
+        )
+    landed = jnp.concatenate(landed_halves, axis=1)
 
     own_pages = page_count // seq_count
     first_page = seq_index * own_pages
@@ -175,10 +189,19 @@
 
 
 def solution(mesh):
+    seq_devices = mesh.devices[:, 0]
+    part_sizes = (
+        len({d.coords[2] for d in seq_devices}),
+        len({d.coords[1] for d in seq_devices}),
+        len({d.core_on_chip for d in seq_devices}),
+    )
+    fine = jax.sharding.Mesh(
+        mesh.devices.reshape(*part_sizes, mesh.devices.shape[1]), (*SEQ_PARTS, "mp")
+    )
     return jax.shard_map(
         local,
-        mesh=mesh,
-        in_specs=(P("seq", None), P("seq", "mp"), P("mp", "seq"), P(), P(), P()),
-        out_specs=P("seq", "mp"),
+        mesh=fine,
+        in_specs=(P(SEQ_PARTS, None), P(SEQ_PARTS, "mp"), P("mp", SEQ_PARTS), P(), P(), P()),
+        out_specs=P(SEQ_PARTS, "mp"),
         check_vma=False,
     )

time: 383 us -> 404 us (1.055)
  waiting for transfers between devices: 172 us -> 99.6 us
  matrix products: 73.8 us -> 108 us
  blocking collectives: 0 us -> 23.7 us
  local copies, waits for them, and re-layouts: 66.5 us -> 85.9 us
  starting transfers between devices: 15.1 us -> 28.9 us
    dot_general x4 -> x8, matrix products: 26.1 us -> 60.9 us  [local(): jnp.einsum('wqk,wkd->wqd', weights, own_values, preferred_element_type=jn...]
    all_to_all x1 -> x2, waiting for transfers between devices: 33.7 us -> 0.66 us  [local(): lax.all_to_all(spread, 'mp', split_axis=1, concat_axis=3, tiled=True)]
    all_gather x1 -> x2, waiting for transfers between devices: 70.3 us -> 40.4 us  [local(): joined = lax.all_gather(joined, name, axis=0)]
    all_gather x0 -> x1, blocking collectives: none -> 23.7 us  [local(): joined = lax.all_gather(joined, name, axis=0)]
    all_to_all x1 -> x2, starting transfers between devices: 10.8 us -> 20.4 us  [local(): lax.all_to_all(sectioned, (*SEQ_PARTS, 'mp'), split_axis=0, concat_axis=0...]
    all_to_all x1 -> x2, waiting for transfers between devices: 67.9 us -> 58.5 us  [local(): lax.all_to_all(sectioned, (*SEQ_PARTS, 'mp'), split_axis=0, concat_axis=0...]
    reshape x4 -> x9, local copies, waits for them, and re-layouts: 15.6 us -> 25 us  [the longest x4 9.79 us: local(): block_out.reshape(page_count, half_tokens, QUARTERS, share_width)]
    transpose x0 -> x1, local copies, waits for them, and re-layouts: none -> 5.62 us  [local(): jnp.transpose(joined, (*reversed(range(len(SEQ_PARTS))), len(SEQ_PARTS),...]
  transfers between devices with their start and end apart: 4 -> 7, of which waited for: 3 -> 5; matrix products, arithmetic and copies ran while one was open for 17% -> 47% of each run, Pallas kernels for 0% -> 0%
where the time goes in v2:
time: 404 us; the launch traced here: 399 us
  matrix products  108 us (27%)
  waiting for transfers between devices  99.6 us (25%)
  local copies, waits for them, and re-layouts  85.9 us (21%)
  other arithmetic  33.9 us (8%)
  starting transfers between devices  28.9 us (7%)
  blocking collectives  23.7 us (6%)
  between operations  19.3 us (5%)
    dot_general x8, matrix products, local(): jnp.einsum('wqk,wkd->wqd', weights, own_values, preferred_element_type=jn...  60.9 us
    all_to_all x2, waiting for transfers between devices, local(): lax.all_to_all(sectioned, (*SEQ_PARTS, 'mp'), split_axis=0, concat_axis=0...  58.5 us
    all_gather x2, waiting for transfers between devices, local(): joined = lax.all_gather(joined, name, axis=0)  40.4 us
    all_gather x1, blocking collectives, local(): joined = lax.all_gather(joined, name, axis=0)  23.7 us
    dot_general x1, matrix products, local(): projected = jnp.dot(normed, fused, preferred_element_type=jnp.float32)  21.3 us
    all_to_all x2, starting transfers between devices, local(): lax.all_to_all(sectioned, (*SEQ_PARTS, 'mp'), split_axis=0, concat_axis=0...  20.4 us
    dot_general x8, matrix products, local(): jnp.einsum('wqd,wkd->wqk', picked, key_block, preferred_element_type=jnp....  14.7 us
    dot_general x2, matrix products, local(): lax.dot_general(gathered, out_full_t, (((1,), (1,)), ((), ())), preferred...  10.8 us
  transfers between devices with their start and end apart: 7, of which 5 were waited for; matrix products, arithmetic and copies ran while one was open for 47% of the time, Pallas kernels for 0%

profile of v2, /device:TPU:1, one launch (start us, length us, event | category | flops | bytes accessed | tf_op | source)
XLA Modules:
  0.0 399.1 jit_solution(6522956245641106566)
XLA Ops:
  7.4 23.7 %all-gather.3 = bf16[8,20,1280]{2,1,0:T(8,128)(2,1)S(1)} all-gather(bf16[1,20,1280]{2,1,0:T(8,128)(2,1)S(1)} %maximum_bitcast_fusion.1), channel_id=2, replica_groups=mesh['z'=8,'y'=4,'core'=2,'mp'=4] {'z'}, dimensions={0}, use_global_device_ids=true | all-gather | bytes 460800 | tf_op jit(solution)/shard_map/all_gather | solution.py:87
  33.9 33.0 %all-gather.10.cloned.1.call-done = bf16[32,20,1280]{2,0,1:T(8,128)(2,1)} async-done(((bf16[8,20,1280]{2,0,1:T(8,128)(2,1)}), bf16[32,20,1280]{2,0,1:T(8,128)(2,1)}) %all-gather.10.cloned.1.call-update) | async-done | bytes 1638416 | tf_op jit(solution)/shard_map/all_gather | solution.py:87
  67.4 6.1 %fusion.8 = f32[4096]{0:T(1024)S(1)} fusion(bf16[4096,1280]{1,0:T(8,128)(2,1)} %param.6), kind=kLoop, calls=%fused_computation.11 | loop fusion | flops 15724544 | bytes 10502144 | tf_op jit(solution)/shard_map/reduce_sum | solution.py:64
  73.6 6.3 %fusion.101 = (f32[4096,80]{0,1:T(8,128)}, f32[4096,80]{0,1:T(8,128)}) fusion(f32[4096,20]{0,1:T(8,128)S(1)} %get-tuple-element.19, f32[4096,20]{0,1:T(8,128)S(1)} %get-tuple-element.18), kind=kLoop, calls=%fused_computation.114 | loop fusion | flops 983040 | bytes 3276800 | tf_op jit(solution)/shard_map/cos | solution.py:27
  79.9 7.3 %all-gather.12.cloned.1.call-done = bf16[8,8,20,1280]{3,1,0,2:T(8,128)(2,1)} async-done(((bf16[4,8,20,1280]{3,1,0,2:T(8,128)(2,1)}), bf16[8,8,20,1280]{3,1,0,2:T(8,128)(2,1)}) %all-gather.12.cloned.1.call-update) | async-done | bytes 3276816 | tf_op jit(solution)/shard_map/all_gather | solution.py:87
  87.2 5.6 %copy.75 = bf16[8,4,2,20,1280]{4,3,2,1,0:T(8,128)(2,1)} copy(bf16[8,4,2,20,1280]{4,0,1,2,3:T(8,128)(2,1)} %bitcast.146) | data formatting | bytes 6553600 | tf_op jit(solution)/shard_map/transpose | solution.py:90
  92.8 4.6 %reshape.667 = bf16[1280,1280]{1,0:T(8,128)(2,1)S(1)} reshape(bf16[8,4,2,20,1280]{4,3,2,1,0:T(8,128)(2,1)} %copy.75) | data formatting | bytes 6553600 | tf_op jit(solution)/shard_map/reshape | solution.py:91
  110.7 21.3 %fusion.10 = f32[4096,1600]{0,1:T(8,128)S(1)} fusion(bf16[1280,1600]{0,1:T(8,128)(2,1)} %constant_dynamic-update-slice_fusion, bf16[4096,1280]{1,0:T(8,128)(2,1)} %param.6, f32[4096]{0:T(1024)S(1)} %add_rsqrt_fusion), kind=kOutput, calls=%fused_computation.13 | convolution fusion | flops 16792944640 | bytes 40812544 | tf_op jit(solution)/shard_map/dot_general | solution.py:120
  134.7 4.7 %fusion.13 = bf16[4096,640]{0,1:T(8,128)(2,1)} fusion(f32[4096,1600]{0,1:T(8,128)S(1)} %fusion.10, f32[4096,80]{0,1:T(8,128)S(1)} %copy-done.2, f32[4096,80]{0,1:T(8,128)S(1)} %copy-done.1), kind=kLoop, calls=%fused_computation.16 | loop fusion | flops 10485760 | bytes 28835840 | tf_op jit(solution)/shard_map/convert_element_type | solution.py:123
  139.4 7.9 %copy.77 = bf16[4096,640]{1,0:T(8,128)(2,1)} copy(bf16[4096,640]{0,1:T(8,128)(2,1)} %fusion.13) | data formatting | bytes 10485760 | tf_op jit(solution)/shard_map/convert_element_type | solution.py:123
  162.9 7.0 %fusion.19 = f32[64,32,320]{2,1,0:T(8,128)} fusion(bf16[64,64,320]{2,1,0:T(8,128)(2,1)S(1)} %bitcast.123, pred[320]{0:T(512)(128)(4,1)S(1)} %broadcast_compare_fusion.2, f32[64,32]{1,0:T(8,128)S(1)} %fusion.171, f32[64,32,64]{2,1,0:T(8,128)} %copy-done.13), kind=kOutput, calls=%fused_computation.34 | convolution fusion | flops 85592128 | bytes 5775680 | tf_op jit(solution)/shard_map/wqk,wkd->wqd/dot_general | solution.py:149
  169.9 7.1 %fusion.23 = f32[64,32,320]{2,1,0:T(8,128)} fusion(bf16[64,64,320]{2,1,0:T(8,128)(2,1)S(1)} %bitcast.124, pred[320]{0:T(512)(128)(4,1)S(1)} %broadcast_compare_fusion.1, f32[64,32]{1,0:T(8,128)S(1)} %fusion.170, f32[64,32,64]{2,1,0:T(8,128)} %copy-done.11), kind=kOutput, calls=%fused_computation.38 | convolution fusion | flops 85592128 | bytes 5775680 | tf_op jit(solution)/shard_map/wqk,wkd->wqd/dot_general | solution.py:149
  176.9 7.1 %fusion.21 = f32[64,32,320]{2,1,0:T(8,128)} fusion(bf16[64,64,320]{2,1,0:T(8,128)(2,1)S(1)} %bitcast.125, pred[320]{0:T(512)(128)(4,1)S(1)} %broadcast_compare_fusion.3, f32[64,32]{1,0:T(8,128)S(1)} %fusion.172, f32[64,32,64]{2,1,0:T(8,128)} %copy-done.9), kind=kOutput, calls=%fused_computation.36 | convolution fusion | flops 85592128 | bytes 5775680 | tf_op jit(solution)/shard_map/wqk,wkd->wqd/dot_general | solution.py:149
  184.1 9.2 %fusion.26 = bf16[64,4,8,1,320]{4,2,1,0,3:T(8,128)(2,1)} fusion(f32[64,32,320]{2,1,0:T(8,128)} %fusion.23, f32[64,32,320]{2,1,0:T(8,128)} %fusion.19, f32[64,32,320]{2,1,0:T(8,128)} %fusion.21, bf16[64,64,320]{2,1,0:T(8,128)(2,1)S(1)} %bitcast.126, pred[320]{0:T(512)(128)(4,1)S(1)} %broadcast_compare_fusion, f32[64,32]{1,0:T(8,128)S(1)} %fusion.173, ...), kind=kOutput, calls=%fused_computation.42 | convolution fusion | flops 88213568 | bytes 12329280 | tf_op jit(solution)/shard_map/wqk,wkd->wqd/dot_general | solution.py:149
  215.7 6.9 %fusion.18 = f32[64,32,320]{2,1,0:T(8,128)} fusion(bf16[64,64,320]{2,1,0:T(8,128)(2,1)S(1)} %bitcast.127, pred[320]{0:T(512)(128)(4,1)S(1)} %broadcast_compare_fusion.2, f32[64,32]{1,0:T(8,128)S(1)} %fusion.167, f32[64,32,64]{2,1,0:T(8,128)} %copy-done.12), kind=kOutput, calls=%fused_computation.33 | convolution fusion | flops 85592128 | bytes 5775680 | tf_op jit(solution)/shard_map/wqk,wkd->wqd/dot_general | solution.py:149
  222.7 7.4 %fusion.22 = f32[64,32,320]{2,1,0:T(8,128)} fusion(bf16[64,64,320]{2,1,0:T(8,128)(2,1)S(1)} %bitcast.128, pred[320]{0:T(512)(128)(4,1)S(1)} %broadcast_compare_fusion.1, f32[64,32]{1,0:T(8,128)S(1)} %fusion.166, f32[64,32,64]{2,1,0:T(8,128)} %copy-done.10), kind=kOutput, calls=%fused_computation.37 | convolution fusion | flops 85592128 | bytes 5775680 | tf_op jit(solution)/shard_map/wqk,wkd->wqd/dot_general | solution.py:149
  230.0 7.0 %fusion.20 = f32[64,32,320]{2,1,0:T(8,128)} fusion(bf16[64,64,320]{2,1,0:T(8,128)(2,1)S(1)} %bitcast.129, pred[320]{0:T(512)(128)(4,1)S(1)} %broadcast_compare_fusion.3, f32[64,32]{1,0:T(8,128)S(1)} %fusion.168, f32[64,32,64]{2,1,0:T(8,128)} %copy-done.8), kind=kOutput, calls=%fused_computation.35 | convolution fusion | flops 85592128 | bytes 5775680 | tf_op jit(solution)/shard_map/wqk,wkd->wqd/dot_general | solution.py:149
  237.0 9.2 %fusion.27 = bf16[64,4,8,1,320]{4,2,1,0,3:T(8,128)(2,1)} fusion(f32[64,32,320]{2,1,0:T(8,128)} %fusion.22, f32[64,32,320]{2,1,0:T(8,128)} %fusion.18, f32[64,32,320]{2,1,0:T(8,128)} %fusion.20, bf16[64,64,320]{2,1,0:T(8,128)(2,1)S(1)} %bitcast.130, pred[320]{0:T(512)(128)(4,1)S(1)} %broadcast_compare_fusion, f32[64,32]{1,0:T(8,128)S(1)} %fusion.169, ...), kind=kOutput, calls=%fused_computation.43 | convolution fusion | flops 88213568 | bytes 12329280 | tf_op jit(solution)/shard_map/wqk,wkd->wqd/dot_general | solution.py:149
  262.0 5.6 %fusion.16 = bf16[512,1280]{1,0:T(8,128)(2,1)} fusion(bf16[512,1280]{1,0:T(8,128)(2,1)} %reshape.675, bf16[1280,1280]{0,1:T(8,128)(2,1)} %all-gather.8.cloned.1.call-done, bf16[64,2,8,1280]{3,2,0,1:T(8,128)(2,1)} %copy_bitcast_fusion), kind=kOutput, calls=%fused_computation.31 | convolution fusion | flops 1679687680 | bytes 7208960 | tf_op jit(solution)/shard_map/dot_general | solution.py:158
  273.2 12.8 %all-to-all-start.1 = ((bf16[256,8,320]{2,1,0:T(8,128)(2,1)}), bf16[256,8,320]{2,1,0:T(8,128)(2,1)S(1)}, u32[]{:S(2)}, u32[]{:S(2)}) async-start(bf16[256,8,320]{2,1,0:T(8,128)(2,1)} %bitcast.33), calls=%async_computation.1 | async-start | bytes 3145728 | tf_op jit(solution)/shard_map/all_to_all | solution.py:169
  292.3 5.2 %fusion.17 = bf16[512,1280]{1,0:T(8,128)(2,1)} fusion(bf16[512,1280]{1,0:T(8,128)(2,1)S(1)} %reshape.679, bf16[1280,1280]{0,1:T(8,128)(2,1)} %all-gather.8.cloned.1.call-done, bf16[64,2,8,1280]{3,2,0,1:T(8,128)(2,1)} %copy_bitcast_fusion), kind=kOutput, calls=%fused_computation.32 | convolution fusion | flops 1679687680 | bytes 7208960 | tf_op jit(solution)/shard_map/dot_general | solution.py:158
  302.4 25.6 %all-to-all-done.1 = bf16[256,8,320]{2,1,0:T(8,128)(2,1)S(1)} async-done(((bf16[256,8,320]{2,1,0:T(8,128)(2,1)}), bf16[256,8,320]{2,1,0:T(8,128)(2,1)S(1)}, u32[]{:S(2)}, u32[]{:S(2)}) %all-to-all-start.1) | async-done | bytes 1310752 | tf_op jit(solution)/shard_map/all_to_all | solution.py:169
  328.1 7.5 %all-to-all-start.3 = ((bf16[256,8,320]{2,1,0:T(8,128)(2,1)}), bf16[256,8,320]{2,1,0:T(8,128)(2,1)}, u32[]{:S(2)}, u32[]{:S(2)}) async-start(bf16[256,8,320]{2,1,0:T(8,128)(2,1)} %bitcast.40), calls=%async_computation.3 | async-start | bytes 3145728 | tf_op jit(solution)/shard_map/all_to_all | solution.py:169
  344.0 32.9 %all-to-all-done.3 = bf16[256,8,320]{2,1,0:T(8,128)(2,1)} async-done(((bf16[256,8,320]{2,1,0:T(8,128)(2,1)}), bf16[256,8,320]{2,1,0:T(8,128)(2,1)}, u32[]{:S(2)}, u32[]{:S(2)}) %all-to-all-start.3) | async-done | bytes 1310752 | tf_op jit(solution)/shard_map/all_to_all | solution.py:169
  (126 shorter events, 108.6 us)
Async XLA Ops:
  6.5 60.4 %all-gather.10.cloned.1.call-start = ((), (), s32[]{:S(2)}) async-start(), calls=%async_computation.5 | async-start | bytes 2048000 | tf_op jit(solution)/shard_map/all_gather | solution.py:87
  32.0 55.2 %all-gather.12.cloned.1.call-start = ((), (), s32[]{:S(2)}) async-start(), calls=%async_computation.6 | async-start | bytes 4915200 | tf_op jit(solution)/shard_map/all_gather | solution.py:87
  66.9 195.1 %all-gather.8.cloned.1.call-start = ((), (), s32[]{:S(2)}) async-start(), calls=%async_computation.4 | async-start | bytes 4096000 | tf_op jit(solution)/shard_map/all_gather | solution.py:109
  100.7 3.3 copy-start.3
  132.0 1.9 copy-start.1
  132.0 2.7 copy-start.2
  151.0 3.7 copy-start
  153.4 7.2 %copy-start.4 = (bf16[64,64,320]{2,1,0:T(8,128)(2,1)}, bf16[64,64,320]{2,1,0:T(8,128)(2,1)S(1)}, u32[]{:S(2)}) copy-start(bf16[64,64,320]{2,1,0:T(8,128)(2,1)S(1)} %slice.86) | copy-start | bytes 7864324
  156.0 2.0 copy-start.9
  158.0 2.0 copy-start.11
  159.9 2.0 copy-start.7
  196.0 52.9 %all-to-all-start = ((bf16[64,4,8,1,320]{4,2,0,3,1:T(8,128)(2,1)}), bf16[64,4,8,1,320]{4,2,0,3,1:T(8,128)(2,1)}, u32[]{:S(2)}, u32[]{:S(2)}) async-start(bf16[64,4,8,1,320]{4,2,0,3,1:T(8,128)(2,1)} %copy.79), calls=%async_computation | async-start | bytes 3145728 | tf_op jit(solution)/shard_map/all_to_all | solution.py:155
  200.4 5.5 %copy-start.5 = (bf16[64,64,320]{2,1,0:T(8,128)(2,1)S(1)}, bf16[64,64,320]{2,1,0:T(8,128)(2,1)}, u32[]{:S(2)}) copy-start(bf16[64,64,320]{2,1,0:T(8,128)(2,1)} %copy-done.4) | copy-start | bytes 7864324
  200.4 10.4 %slice-start = ((s8[5242880]{0:T(1024)(128)(4,1)}), s8[4194304]{0:T(1024)(128)(4,1)S(1)}, s32[]{:S(2)}) async-start(s8[5242880]{0:T(1024)(128)(4,1)} %bitcast.140), calls=%async_computation.7 | async-start | bytes 8388608
  204.2 1.0 copy-start.8
  205.9 4.9 %slice-start.1 = ((s8[5242880]{0:T(1024)(128)(4,1)}), s8[1048576]{0:T(1024)(128)(4,1)S(1)}, s32[]{:S(2)}) async-start(s8[5242880]{0:T(1024)(128)(4,1)} %bitcast.140), calls=%async_computation.8 | async-start | bytes 2097152
  209.1 1.0 copy-start.10
  212.1 2.0 copy-start.6
  214.1 1.0 copy-start.12
  248.9 24.3 %all-to-all-start.2 = ((bf16[64,4,8,1,320]{4,2,0,3,1:T(8,128)(2,1)}), bf16[64,4,8,1,320]{4,2,0,3,1:T(8,128)(2,1)S(1)}, u32[]{:S(2)}, u32[]{:S(2)}) async-start(bf16[64,4,8,1,320]{4,2,0,3,1:T(8,128)(2,1)} %copy.83), calls=%async_computation.2 | async-start | bytes 3145728 | tf_op jit(solution)/shard_map/all_to_all | solution.py:155
  273.2 54.9 %all-to-all-start.1 = ((bf16[256,8,320]{2,1,0:T(8,128)(2,1)}), bf16[256,8,320]{2,1,0:T(8,128)(2,1)S(1)}, u32[]{:S(2)}, u32[]{:S(2)}) async-start(bf16[256,8,320]{2,1,0:T(8,128)(2,1)} %bitcast.33), calls=%async_computation.1 | async-start | bytes 3145728 | tf_op jit(solution)/shard_map/all_to_all | solution.py:169
  301.0 34.6 %copy-start.14 = (s32[64]{0:T(128)S(1)}, s32[64]{0:T(128)}, u32[]{:S(2)}) copy-start(s32[64]{0:T(128)} %param.10) | copy-start | bytes 772
  301.0 38.1 %copy-start.15 = (s32[64]{0:T(128)S(1)}, s32[64]{0:T(128)}, u32[]{:S(2)}) copy-start(s32[64]{0:T(128)} %param.9) | copy-start | bytes 772
  328.1 48.8 %all-to-all-start.3 = ((bf16[256,8,320]{2,1,0:T(8,128)(2,1)}), bf16[256,8,320]{2,1,0:T(8,128)(2,1)}, u32[]{:S(2)}, u32[]{:S(2)}) async-start(bf16[256,8,320]{2,1,0:T(8,128)(2,1)} %bitcast.40), calls=%async_computation.3 | async-start | bytes 3145728 | tf_op jit(solution)/shard_map/all_to_all | solution.py:169
  (1 other events, 1.0 us)
Sparse Core Ops, SparseCore 0:
  32.1 34.7 all-gather.9
  68.7 18.4 all-gather.11
  105.5 43.4 all-gather.7

commit v3 on v1

--- a/solution.py
+++ b/solution.py
@@ -120,21 +120,23 @@
     values = projected[:, 4 * width :].astype(jnp.bfloat16).reshape(windows, window_tokens, width)
 
     lane_head = jnp.arange(width, dtype=jnp.int32) // HD
+    head_mask = (jnp.arange(heads, dtype=jnp.int32)[:, None] == lane_head[None, :])[None, :, None, :]
+    spread_keys = jnp.where(head_mask, key_block[:, None], jnp.zeros_like(key_block[:, None]))
+    spread_keys = spread_keys.reshape(windows, heads * window_tokens, width)
+    spread_values = jnp.where(head_mask, values[:, None], jnp.zeros_like(values[:, None]))
+    spread_values = spread_values.reshape(windows, heads * window_tokens, width)
     scale = 1.0 / (HD ** 0.5)
-    mixed = jnp.zeros((windows, window_tokens, width), jnp.float32)
-    for head in range(heads):
-        mask = lane_head == head
-        picked = jnp.where(mask, queries, jnp.zeros_like(queries))
-        scores = jnp.einsum(
-            "wqd,wkd->wqk", picked, key_block, preferred_element_type=jnp.float32
-        ) * scale
-        row_max = jnp.max(scores, axis=-1, keepdims=True)
-        lifted = jnp.exp(scores - row_max)
-        weights = (lifted / jnp.sum(lifted, axis=-1, keepdims=True)).astype(jnp.bfloat16)
-        own_values = jnp.where(mask, values, jnp.zeros_like(values))
-        mixed = mixed + jnp.einsum(
-            "wqk,wkd->wqd", weights, own_values, preferred_element_type=jnp.float32
-        )
+    scores = jnp.einsum(
+        "wqd,wkd->wqk", queries, spread_keys, preferred_element_type=jnp.float32
+    ) * scale
+    scores = scores.reshape(windows, window_tokens, heads, window_tokens)
+    row_max = jnp.max(scores, axis=-1, keepdims=True)
+    lifted = jnp.exp(scores - row_max)
+    weights = (lifted / jnp.sum(lifted, axis=-1, keepdims=True)).astype(jnp.bfloat16)
+    weights = weights.reshape(windows, window_tokens, heads * window_tokens)
+    mixed = jnp.einsum(
+        "wqk,wkd->wqd", weights, spread_values, preferred_element_type=jnp.float32
+    )
     mixed = mixed.astype(jnp.bfloat16)
 
     spread = mixed.reshape(windows, QUARTERS, quarter_tokens, 1, width)

time: 383 us -> 424 us (1.11)
  local copies, waits for them, and re-layouts: 66.5 us -> 109 us
  other arithmetic: 32.3 us -> 56 us
  matrix products: 73.8 us -> 50.6 us
    dot_general x8 -> x2, matrix products: 45.4 us -> 22.1 us  [the longest x1 11.6 us: local(): jnp.einsum('wqd,wkd->wqk', queries, spread_keys, preferred_element_type=j...]
    div x0 -> x2, local copies, waits for them, and re-layouts: none -> 15.7 us  [local(): lifted / jnp.sum(lifted, axis=-1, keepdims=True)]
    sub x0 -> x2, local copies, waits for them, and re-layouts: none -> 15.6 us  [local(): lifted = jnp.exp(scores - row_max)]
    reduce_sum x0 -> x1, other arithmetic: none -> 10.9 us  [local(): jnp.sum(lifted, axis=-1, keepdims=True)]
    select_n x0 -> x2, other arithmetic: none -> 10.8 us  [the longest x1 10.8 us: local(): jnp.where(head_mask, key_block[:, None], jnp.zeros_like(key_block[:, None]))]
    reshape x0 -> x1, local copies, waits for them, and re-layouts: none -> 8.12 us  [local(): scores = scores.reshape(windows, window_tokens, heads, window_tokens)]
    reduce_max x0 -> x1, other arithmetic: none -> 7.97 us  [local(): row_max = jnp.max(scores, axis=-1, keepdims=True)]
    sub x4 -> x0, other arithmetic: 5.9 us -> none  [local(): lifted = jnp.exp(scores - row_max)]
  transfers between devices with their start and end apart: 4 -> 4, of which waited for: 3 -> 3; matrix products, arithmetic and copies ran while one was open for 17% -> 30% of each run, Pallas kernels for 0% -> 0%
where the time goes in v3:
time: 424 us; the launch traced here: 419 us
  waiting for transfers between devices  172 us (41%)
  local copies, waits for them, and re-layouts  109 us (26%)
  other arithmetic  56 us (13%)
  matrix products  50.6 us (12%)
  between operations  19.1 us (5%)
  starting transfers between devices  12.3 us (3%)
    all_gather x1, waiting for transfers between devices, local(): lax.all_gather(jnp.concatenate([w_qkv, w_out.T], axis=1), 'seq', axis=0,...  70.3 us
    all_to_all x1, waiting for transfers between devices, local(): lax.all_to_all(sectioned, ('seq', 'mp'), split_axis=0, concat_axis=0, til...  67.8 us
    all_to_all x1, waiting for transfers between devices, local(): lax.all_to_all(spread, 'mp', split_axis=1, concat_axis=3, tiled=True)  33.6 us
    dot_general x1, matrix products, local(): projected = jnp.dot(normed, fused, preferred_element_type=jnp.float32)  21.3 us
    div x2, local copies, waits for them, and re-layouts, local(): lifted / jnp.sum(lifted, axis=-1, keepdims=True)  15.7 us
    sub x2, local copies, waits for them, and re-layouts, local(): lifted = jnp.exp(scores - row_max)  15.6 us
    dot_general x1, matrix products, local(): jnp.einsum('wqd,wkd->wqk', queries, spread_keys, preferred_element_type=j...  11.6 us
    reduce_sum x1, other arithmetic, local(): jnp.sum(lifted, axis=-1, keepdims=True)  10.9 us
  transfers between devices with their start and end apart: 4, of which 3 were waited for; matrix products, arithmetic and copies ran while one was open for 30% of the time, Pallas kernels for 0%

profile of v3, /device:TPU:1, one launch (start us, length us, event | category | flops | bytes accessed | tf_op | source)
XLA Modules:
  0.0 418.9 jit_solution(11014662872426147819)
XLA Ops:
  10.3 6.1 %fusion = f32[4096]{0:T(1024)S(1)} fusion(bf16[4096,1280]{1,0:T(8,128)(2,1)} %param.6), kind=kLoop, calls=%fused_computation.3 | loop fusion | flops 15724544 | bytes 10502144 | tf_op jit(solution)/shard_map/reduce_sum | solution.py:62
  16.5 6.2 %fusion.15 = (f32[4096,80]{0,1:T(8,128)}, f32[4096,80]{0,1:T(8,128)}) fusion(f32[4096,20]{0,1:T(8,128)S(1)} %get-tuple-element.21, f32[4096,20]{0,1:T(8,128)S(1)} %get-tuple-element.20), kind=kLoop, calls=%fused_computation.26 | loop fusion | flops 983040 | bytes 3276800 | tf_op jit(solution)/shard_map/cos | solution.py:25
  22.8 70.3 %all-gather.6.cloned.1.call-done = bf16[64,20,1280]{2,1,0:T(8,128)(2,1)} async-done(((bf16[1,20,1280]{2,1,0:T(8,128)(2,1)}), bf16[64,20,1280]{2,1,0:T(8,128)(2,1)}) %all-gather.6.cloned.1.call-update) | async-done | bytes 3276816 | tf_op jit(solution)/shard_map/all_gather | solution.py:83
  93.1 4.6 %reshape.701 = bf16[1280,1280]{1,0:T(8,128)(2,1)S(1)} reshape(bf16[64,20,1280]{2,1,0:T(8,128)(2,1)} %all-gather.6.cloned.1.call-done) | data formatting | bytes 6553600
  109.5 21.3 %fusion.2 = f32[4096,1600]{0,1:T(8,128)S(1)} fusion(bf16[1280,1600]{0,1:T(8,128)(2,1)} %constant_dynamic-update-slice_fusion, bf16[4096,1280]{1,0:T(8,128)(2,1)} %param.6, f32[4096]{0:T(1024)S(1)} %add_rsqrt_fusion), kind=kOutput, calls=%fused_computation.7 | convolution fusion | flops 16792944640 | bytes 40812544 | tf_op jit(solution)/shard_map/dot_general | solution.py:114
  138.1 7.8 %copy.33 = bf16[4096,640]{1,0:T(8,128)(2,1)} copy(bf16[4096,640]{0,1:T(8,128)(2,1)} %fusion.5) | data formatting | bytes 10485760 | tf_op jit(solution)/shard_map/convert_element_type | solution.py:117
  156.4 10.8 %bitcast_select_fusion.1 = (bf16[64,256,320]{2,1,0:T(8,128)(2,1)}, bf16[64,256,320]{2,1,0:T(8,128)(2,1)}) fusion(pred[256,320]{1,0:T(8,128)(4,1)S(1)} %bitcast.75, bf16[64,64,320]{2,1,0:T(8,128)(2,1)S(1)} %slice.70, bf16[64,64,320]{2,1,0:T(8,128)(2,1)} %bitcast.67), kind=kLoop, calls=%fused_computation.6 | loop fusion | flops 10485760 | bytes 26296320 | tf_op jit(solution)/shard_map/jit(_where)/select_n | solution.py:124
  167.2 11.6 %fusion.11 = f32[64,64,256]{2,1,0:T(8,128)} fusion(bf16[64,256,320]{2,1,0:T(8,128)(2,1)} %get-tuple-element.18, bf16[64,64,640]{2,1,0:T(8,128)(2,1)} %bitcast.60), kind=kOutput, calls=%fused_computation.23 | convolution fusion | flops 672137216 | bytes 19922944 | tf_op jit(solution)/shard_map/wqd,wkd->wqk/dot_general | solution.py:129
  178.9 8.1 %reshape.684 = f32[64,64,4,64]{3,2,1,0:T(4,128)} reshape(f32[64,64,256]{2,1,0:T(8,128)} %fusion.11) | data formatting | bytes 8388608 | tf_op jit(solution)/shard_map/reshape | solution.py:132
  187.0 8.0 %reduce_max.9 = f32[64,64,4]{2,1,0:T(8,128)S(1)} reduce(f32[64,64,4,64]{3,2,1,0:T(4,128)} %reshape.684, f32[]{:T(128)} %constant.206.clone.1), dimensions={3}, to_apply=%region_3.4 | reduce | flops 1032192 | bytes 4259844 | tf_op jit(solution)/shard_map/reduce_max | solution.py:133
  194.9 10.9 %exponential_reduce_fusion = f32[64,64,4]{2,1,0:T(8,128)S(1)} fusion(f32[64,64,4,64]{3,2,1,0:T(4,128)} %reshape.684, f32[64,64,4]{2,1,0:T(8,128)S(1)} %reduce_max.9), kind=kLoop, calls=%fused_computation.13 | loop fusion | flops 2080768 | bytes 4325376 | tf_op jit(solution)/shard_map/reduce_sum | solution.py:135
  205.9 7.1 %div.175 = f32[64,64,4,64]{3,2,1,0:T(4,128)} broadcast(f32[64,64,4]{2,1,0:T(8,128)S(1)} %exponential_reduce_fusion), dimensions={0,1,2} | broadcast | bytes 4259840 | tf_op jit(solution)/shard_map/div | solution.py:135
  213.0 8.6 %div.176 = f32[64,64,256]{2,1,0:T(8,128)} reshape(f32[64,64,4,64]{3,2,1,0:T(4,128)} %div.175) | data formatting | bytes 8388608 | tf_op jit(solution)/shard_map/div | solution.py:135
  221.6 7.1 %sub.78 = f32[64,64,4,64]{3,2,1,0:T(4,128)} broadcast(f32[64,64,4]{2,1,0:T(8,128)S(1)} %reduce_max.9), dimensions={0,1,2} | broadcast | bytes 4259840 | tf_op jit(solution)/shard_map/sub | solution.py:134
  228.6 8.6 %sub.79 = f32[64,64,256]{2,1,0:T(8,128)} reshape(f32[64,64,4,64]{3,2,1,0:T(4,128)} %sub.78) | data formatting | bytes 8388608 | tf_op jit(solution)/shard_map/sub | solution.py:134
  237.2 10.5 %convolution_convert_fusion = bf16[64,64,320]{2,1,0:T(8,128)(2,1)S(1)} fusion(bf16[64,256,320]{2,1,0:T(8,128)(2,1)} %get-tuple-element.19, f32[64,64,256]{2,1,0:T(8,128)} %div.176, f32[64,64,256]{2,1,0:T(8,128)} %fusion.11, f32[64,64,256]{2,1,0:T(8,128)} %sub.79), kind=kOutput, calls=%fused_computation.22 | convolution fusion | flops 675545088 | bytes 25690112 | tf_op jit(solution)/shard_map/wqk,wkd->wqd/dot_general | solution.py:137
  257.2 33.6 %all-to-all-done = bf16[64,4,16,1,320]{4,2,0,3,1:T(8,128)(2,1)S(1)} async-done(((bf16[64,4,16,1,320]{4,2,0,3,1:T(8,128)(2,1)}), bf16[64,4,16,1,320]{4,2,0,3,1:T(8,128)(2,1)S(1)}, u32[]{:S(2)}, u32[]{:S(2)}) %all-to-all-start) | async-done | bytes 2621472 | tf_op jit(solution)/shard_map/all_to_all | solution.py:143
  290.9 5.7 %copy.38 = bf16[64,1,16,4,1,320]{5,3,2,0,4,1:T(4,128)(2,1)} copy(bf16[64,1,16,4,1,320]{5,2,0,3,4,1:T(8,128)(2,1)S(1)} %bitcast.66) | data formatting | bytes 5242880 | tf_op jit(solution)/shard_map/all_to_all | solution.py:143
  296.6 5.1 %reshape.686 = bf16[1024,1280]{1,0:T(8,128)(2,1)S(1)} reshape(bf16[64,1,16,4,1,320]{5,3,2,0,4,1:T(4,128)(2,1)} %copy.38) | data formatting | bytes 5242880 | tf_op jit(solution)/shard_map/reshape | solution.py:144
  301.7 7.1 %fusion.7 = bf16[1024,1280]{1,0:T(8,128)(2,1)} fusion(bf16[1024,1280]{1,0:T(8,128)(2,1)} %bitcast.74, bf16[1024,1280]{1,0:T(8,128)(2,1)S(1)} %reshape.686, bf16[1280,1280]{0,1:T(8,128)(2,1)} %all-gather.4.cloned.1.call-done), kind=kOutput, calls=%fused_computation.16 | convolution fusion | flops 3359375360 | bytes 11141120 | tf_op jit(solution)/shard_map/dot_general | solution.py:146
  308.9 6.1 %reshape.687 = bf16[64,16,4,320]{3,2,1,0:T(4,128)(2,1)S(1)} reshape(bf16[1024,1280]{1,0:T(8,128)(2,1)} %fusion.7) | data formatting | bytes 5242880 | tf_op jit(solution)/shard_map/reshape | solution.py:155
  317.4 8.1 %all-to-all-start.1 = ((bf16[256,16,320]{2,1,0:T(8,128)(2,1)}), bf16[256,16,320]{2,1,0:T(8,128)(2,1)S(1)}, u32[]{:S(2)}, u32[]{:S(2)}) async-start(bf16[256,16,320]{2,1,0:T(8,128)(2,1)} %bitcast.65), calls=%async_computation.1 | async-start | bytes 6291456 | tf_op jit(solution)/shard_map/all_to_all | solution.py:159
  333.6 67.8 %all-to-all-done.1 = bf16[256,16,320]{2,1,0:T(8,128)(2,1)S(1)} async-done(((bf16[256,16,320]{2,1,0:T(8,128)(2,1)}), bf16[256,16,320]{2,1,0:T(8,128)(2,1)S(1)}, u32[]{:S(2)}, u32[]{:S(2)}) %all-to-all-start.1) | async-done | bytes 2621472 | tf_op jit(solution)/shard_map/all_to_all | solution.py:159
  404.1 5.0 %fusion.10 = bf16[4096,320]{1,0:T(8,128)(2,1)S(1)} fusion(bf16[256,16,320]{2,1,0:T(8,128)(2,1)} %gather_fusion, pred[4096]{0:T(1024)(128)(4,1)S(1)} %broadcast_in_dim.165, pred[4096]{0:T(1024)(128)(4,1)S(1)} %broadcast_in_dim.159), kind=kLoop, calls=%fused_computation.21 | loop fusion | flops 2621440 | bytes 5251072 | tf_op jit(solution)/shard_map/vmap(jit(_where))/select_n | solution.py:173
  (65 shorter events, 53.5 us)
Async XLA Ops:
  6.5 86.5 %all-gather.6.cloned.1.call-start = ((), (), s32[]{:S(2)}) async-start(), calls=%async_computation.3 | async-start | bytes 3993600 | tf_op jit(solution)/shard_map/all_gather | solution.py:83
  8.1 293.7 %all-gather.4.cloned.1.call-start = ((), (), s32[]{:S(2)}) async-start(), calls=%async_computation.2 | async-start | bytes 4096000 | tf_op jit(solution)/shard_map/all_gather | solution.py:103
  130.8 1.9 copy-start
  130.8 2.6 copy-start.1
  249.7 41.2 %all-to-all-start = ((bf16[64,4,16,1,320]{4,2,0,3,1:T(8,128)(2,1)}), bf16[64,4,16,1,320]{4,2,0,3,1:T(8,128)(2,1)S(1)}, u32[]{:S(2)}, u32[]{:S(2)}) async-start(bf16[64,4,16,1,320]{4,2,0,3,1:T(8,128)(2,1)} %copy.37), calls=%async_computation | async-start | bytes 6291456 | tf_op jit(solution)/shard_map/all_to_all | solution.py:143
  317.4 8.1 %copy-start.2 = (s32[64]{0:T(128)S(1)}, s32[64]{0:T(128)}, u32[]{:S(2)}) copy-start(s32[64]{0:T(128)} %param.10) | copy-start | bytes 772
  317.4 11.3 %copy-start.3 = (s32[64]{0:T(128)S(1)}, s32[64]{0:T(128)}, u32[]{:S(2)}) copy-start(s32[64]{0:T(128)} %param.9) | copy-start | bytes 772
  317.4 84.1 %all-to-all-start.1 = ((bf16[256,16,320]{2,1,0:T(8,128)(2,1)}), bf16[256,16,320]{2,1,0:T(8,128)(2,1)S(1)}, u32[]{:S(2)}, u32[]{:S(2)}) async-start(bf16[256,16,320]{2,1,0:T(8,128)(2,1)} %bitcast.65), calls=%async_computation.1 | async-start | bytes 6291456 | tf_op jit(solution)/shard_map/all_to_all | solution.py:159
Sparse Core Ops, SparseCore 0:
  10.0 83.0 all-gather.5
  156.5 39.7 all-gather.3

commit v4 on v1

--- a/solution.py
+++ b/solution.py
@@ -80,26 +80,25 @@
     model_width = patches.shape[1]
     windows = patches.shape[0] // window_tokens
 
-    joined = lax.all_gather(
-        jnp.concatenate([w_qkv, w_out.T], axis=1), "seq", axis=0, tiled=True
-    )
-    qkv = joined[:, : w_qkv.shape[1]]
-    out_rows_t = joined[:, w_qkv.shape[1] :]
-    heads = qkv.shape[1] // (3 * HD)
-    qkv = qkv.reshape(model_width, heads, 3, HD)
+    own_rows = w_qkv.shape[0]
+    heads = w_qkv.shape[1] // (3 * HD)
+    qkv = w_qkv.reshape(own_rows, heads, 3, HD)
     w_q = qkv[:, :, 0]
     w_k = qkv[:, :, 1]
-    w_v = qkv[:, :, 2].reshape(model_width, heads * HD)
-    fused = jnp.concatenate(
+    fused_rows = jnp.concatenate(
         [
-            w_q.reshape(model_width, heads * HD),
-            w_k.reshape(model_width, heads * HD),
-            rotated_columns(w_q).reshape(model_width, heads * HD),
-            rotated_columns(w_k).reshape(model_width, heads * HD),
-            w_v,
+            w_q.reshape(own_rows, heads * HD),
+            w_k.reshape(own_rows, heads * HD),
+            rotated_columns(w_q).reshape(own_rows, heads * HD),
+            rotated_columns(w_k).reshape(own_rows, heads * HD),
+            qkv[:, :, 2].reshape(own_rows, heads * HD),
+            w_out.T,
         ],
         axis=1,
     )
+    joined = lax.all_gather(fused_rows, "seq", axis=0, tiled=True)
+    fused = joined[:, : 5 * heads * HD]
+    out_rows_t = joined[:, 5 * heads * HD :]
     out_full_t = lax.all_gather(out_rows_t, "mp", axis=1, tiled=True)
 
     slot_numbers = seq_index * slots_held + jnp.arange(slots_held, dtype=jnp.int32)

time: 383 us -> 382 us (level)
    dot_general x4, matrix products: 19.2 us -> 9.45 us  [local(): jnp.einsum('wqd,wkd->wqk', picked, key_block, preferred_element_type=jnp....]
    dot_general x4, matrix products: 26.1 us -> 35.8 us  [local(): jnp.einsum('wqk,wkd->wqd', weights, own_values, preferred_element_type=jn...]
    convert_element_type x1, other arithmetic: 4.69 us -> 10.4 us  [local(): turned.astype(jnp.bfloat16).reshape(windows, window_tokens, 2 * width)]
    slice x5 -> x3, local copies, waits for them, and re-layouts: 9.02 us -> 5.21 us  [the longest x2 4.81 us: local(): out_rows_t = joined[:, 5 * heads * HD:]]
    unnamed x23 -> x18, local copies, waits for them, and re-layouts: 10.6 us -> 8.29 us
  transfers between devices with their start and end apart: 4 -> 4, of which waited for: 3 -> 3; matrix products, arithmetic and copies ran while one was open for 17% -> 35% of each run, Pallas kernels for 0% -> 0%
where the time goes in v4:
time: 382 us; the launch traced here: 377 us
  waiting for transfers between devices  173 us (45%)
  matrix products  76.2 us (20%)
  local copies, waits for them, and re-layouts  64.9 us (17%)
  other arithmetic  31.8 us (8%)
  between operations  19.1 us (5%)
  starting transfers between devices  11.8 us (3%)
    all_gather x1, waiting for transfers between devices, local(): joined = lax.all_gather(fused_rows, 'seq', axis=0, tiled=True)  71.3 us
    all_to_all x1, waiting for transfers between devices, local(): lax.all_to_all(sectioned, ('seq', 'mp'), split_axis=0, concat_axis=0, til...  67.9 us
    dot_general x4, matrix products, local(): jnp.einsum('wqk,wkd->wqd', weights, own_values, preferred_element_type=jn...  35.8 us
    all_to_all x1, waiting for transfers between devices, local(): lax.all_to_all(spread, 'mp', split_axis=1, concat_axis=3, tiled=True)  33.7 us
    dot_general x1, matrix products, local(): projected = jnp.dot(normed, fused, preferred_element_type=jnp.float32)  23.8 us
    convert_element_type x1, other arithmetic, local(): turned.astype(jnp.bfloat16).reshape(windows, window_tokens, 2 * width)  10.4 us
    dot_general x4, matrix products, local(): jnp.einsum('wqd,wkd->wqk', picked, key_block, preferred_element_type=jnp....  9.45 us
    reshape x2, local copies, waits for them, and re-layouts, local(): block_out.reshape(page_count, quarter_tokens, QUARTERS, share_width)  8.5 us
  transfers between devices with their start and end apart: 4, of which 3 were waited for; matrix products, arithmetic and copies ran while one was open for 35% of the time, Pallas kernels for 0%

profile of v4, /device:TPU:1, one launch (start us, length us, event | category | flops | bytes accessed | tf_op | source)
XLA Modules:
  0.0 376.8 jit_solution(8470830462252085921)
XLA Ops:
  12.5 6.1 %fusion.4 = f32[4096]{0:T(1024)S(1)} fusion(bf16[4096,1280]{1,0:T(8,128)(2,1)} %param.6), kind=kLoop, calls=%fused_computation.7 | loop fusion | flops 15724544 | bytes 10502144 | tf_op jit(solution)/shard_map/reduce_sum | solution.py:62
  18.7 4.8 %fusion.69 = (f32[4096,80]{0,1:T(8,128)S(1)}, f32[4096,80]{0,1:T(8,128)S(1)}) fusion(f32[4096,20]{0,1:T(8,128)S(1)} %get-tuple-element.19, f32[4096,20]{0,1:T(8,128)S(1)} %get-tuple-element.18), kind=kLoop, calls=%fused_computation.88 | loop fusion | flops 983040 | bytes 3276800 | tf_op jit(solution)/shard_map/cos | solution.py:25
  23.5 71.3 %all-gather.6.cloned.1.call-done = bf16[64,20,1920]{2,1,0:T(8,128)(2,1)} async-done(((bf16[1,20,1920]{2,1,0:T(8,128)(2,1)}), bf16[64,20,1920]{2,1,0:T(8,128)(2,1)}) %all-gather.6.cloned.1.call-update) | async-done | bytes 4915216 | tf_op jit(solution)/shard_map/all_gather | solution.py:99
  94.8 7.5 %reshape.661 = bf16[1280,1920]{1,0:T(8,128)(2,1)} reshape(bf16[64,20,1920]{2,1,0:T(8,128)(2,1)} %all-gather.6.cloned.1.call-done) | data formatting | bytes 9830400
  107.2 23.8 %fusion.6 = f32[4096,1600]{0,1:T(8,128)} fusion(bf16[4096,1280]{1,0:T(8,128)(2,1)} %param.6, f32[4096]{0:T(1024)S(1)} %add_rsqrt_fusion, bf16[1280,1920]{1,0:T(8,128)(2,1)} %reshape.661), kind=kOutput, calls=%fused_computation.9 | convolution fusion | flops 16792944640 | bytes 40976384 | tf_op jit(solution)/shard_map/dot_general | solution.py:113
  131.0 4.4 %slice.125 = bf16[4096,320]{0,1:T(8,128)(2,1)} slice(f32[4096,1600]{0,1:T(8,128)} %fusion.6), slice={[0:4096], [1280:1600]} | slice | bytes 5242880 | tf_op jit(solution)/shard_map/slice | solution.py:119
  135.4 10.4 %fusion.9 = bf16[4096,640]{0,1:T(8,128)(2,1)} fusion(f32[4096,1600]{0,1:T(8,128)} %fusion.6, f32[4096,80]{0,1:T(8,128)S(1)} %get-tuple-element.11, f32[4096,80]{0,1:T(8,128)S(1)} %get-tuple-element.10), kind=kLoop, calls=%fused_computation.12 | loop fusion | flops 10485760 | bytes 28835840 | tf_op jit(solution)/shard_map/convert_element_type | solution.py:116
  145.8 7.9 %copy.54 = bf16[4096,640]{1,0:T(8,128)(2,1)} copy(bf16[4096,640]{0,1:T(8,128)(2,1)} %fusion.9) | data formatting | bytes 10485760 | tf_op jit(solution)/shard_map/convert_element_type | solution.py:116
  153.7 3.6 copy.55
  157.3 5.4 %fusion.20 = f32[64,64,64]{1,2,0:T(8,128)S(1)} fusion(pred[320]{0:T(512)(128)(4,1)S(1)} %broadcast_compare_fusion.1, bf16[64,64,640]{2,1,0:T(8,128)(2,1)} %bitcast.54), kind=kOutput, calls=%fused_computation.28 | convolution fusion | flops 169082880 | bytes 7340352 | tf_op jit(solution)/shard_map/wqd,wkd->wqk/dot_general | solution.py:127
  170.2 5.4 %fusion.22 = f32[64,64,320]{2,1,0:T(8,128)} fusion(bf16[64,64,320]{2,1,0:T(8,128)(2,1)S(1)} %bitcast.50, pred[320]{0:T(512)(128)(4,1)S(1)} %broadcast_compare_fusion.3, f32[64,64]{1,0:T(8,128)S(1)} %fusion.127, f32[64,64,64]{1,2,0:T(8,128)} %copy-done.7), kind=kOutput, calls=%fused_computation.30 | convolution fusion | flops 170135616 | bytes 8929600 | tf_op jit(solution)/shard_map/wqk,wkd->wqd/dot_general | solution.py:134
  175.6 5.4 %fusion.14 = f32[64,64,320]{2,1,0:T(8,128)} fusion(bf16[64,64,320]{2,1,0:T(8,128)(2,1)S(1)} %bitcast.51, pred[320]{0:T(512)(128)(4,1)S(1)} %broadcast_compare_fusion, f32[64,64]{1,0:T(8,128)S(1)} %fusion.125, f32[64,64,64]{1,2,0:T(8,128)} %copy-done.6), kind=kOutput, calls=%fused_computation.22 | convolution fusion | flops 170135616 | bytes 8929600 | tf_op jit(solution)/shard_map/wqk,wkd->wqd/dot_general | solution.py:134
  180.9 5.3 %fusion.18 = f32[64,64,320]{2,1,0:T(8,128)} fusion(bf16[64,64,320]{2,1,0:T(8,128)(2,1)S(1)} %bitcast.52, pred[320]{0:T(512)(128)(4,1)S(1)} %broadcast_compare_fusion.1, f32[64,64]{1,0:T(8,128)S(1)} %fusion.126, f32[64,64,64]{1,2,0:T(8,128)} %copy-done.5), kind=kOutput, calls=%fused_computation.26 | convolution fusion | flops 170135616 | bytes 8929600 | tf_op jit(solution)/shard_map/wqk,wkd->wqd/dot_general | solution.py:134
  186.3 19.7 %add_convert_fusion = bf16[64,64,320]{2,1,0:T(8,128)(2,1)S(1)} fusion(f32[64,64,320]{2,1,0:T(8,128)} %fusion.14, f32[64,64,320]{2,1,0:T(8,128)} %fusion.18, f32[64,64,320]{2,1,0:T(8,128)} %fusion.22, bf16[64,64,320]{2,1,0:T(8,128)(2,1)} %bitcast.53, pred[320]{0:T(512)(128)(4,1)S(1)} %broadcast_compare_fusion.2, f32[64,64]{1,0:T(8,128)S(1)} %fusion.128, ...), kind=kOutput, calls=%fused_computation.15 | convolution fusion | flops 175378496 | bytes 22036800 | tf_op jit(solution)/shard_map/wqk,wkd->wqd/dot_general | solution.py:134
  208.0 3.9 %all-to-all-start = ((bf16[64,4,16,1,320]{4,2,0,3,1:T(8,128)(2,1)}), bf16[64,4,16,1,320]{4,2,0,3,1:T(8,128)(2,1)S(1)}, u32[]{:S(2)}, u32[]{:S(2)}) async-start(bf16[64,4,16,1,320]{4,2,0,3,1:T(8,128)(2,1)} %copy.60), calls=%async_computation | async-start | bytes 6291456 | tf_op jit(solution)/shard_map/all_to_all | solution.py:140
  211.9 3.4 constant_dynamic-slice_fusion
  215.3 33.7 %all-to-all-done = bf16[64,4,16,1,320]{4,2,0,3,1:T(8,128)(2,1)S(1)} async-done(((bf16[64,4,16,1,320]{4,2,0,3,1:T(8,128)(2,1)}), bf16[64,4,16,1,320]{4,2,0,3,1:T(8,128)(2,1)S(1)}, u32[]{:S(2)}, u32[]{:S(2)}) %all-to-all-start) | async-done | bytes 2621472 | tf_op jit(solution)/shard_map/all_to_all | solution.py:140
  249.0 5.7 %copy.61 = bf16[64,1,16,4,1,320]{5,3,2,0,4,1:T(4,128)(2,1)} copy(bf16[64,1,16,4,1,320]{5,2,0,3,4,1:T(8,128)(2,1)S(1)} %bitcast.48) | data formatting | bytes 5242880 | tf_op jit(solution)/shard_map/all_to_all | solution.py:140
  254.7 5.1 %reshape.646 = bf16[1024,1280]{1,0:T(8,128)(2,1)S(1)} reshape(bf16[64,1,16,4,1,320]{5,3,2,0,4,1:T(4,128)(2,1)} %copy.61) | data formatting | bytes 5242880 | tf_op jit(solution)/shard_map/reshape | solution.py:141
  259.8 7.1 %fusion.11 = bf16[1024,1280]{1,0:T(8,128)(2,1)} fusion(bf16[1024,1280]{1,0:T(8,128)(2,1)} %bitcast.58, bf16[1024,1280]{1,0:T(8,128)(2,1)S(1)} %reshape.646, bf16[1280,1280]{0,1:T(8,128)(2,1)} %all-gather.4.cloned.1.call-done), kind=kOutput, calls=%fused_computation.18 | convolution fusion | flops 3359375360 | bytes 11141120 | tf_op jit(solution)/shard_map/dot_general | solution.py:143
  267.0 6.1 %reshape.647 = bf16[64,16,4,320]{3,2,1,0:T(4,128)(2,1)S(1)} reshape(bf16[1024,1280]{1,0:T(8,128)(2,1)} %fusion.11) | data formatting | bytes 5242880 | tf_op jit(solution)/shard_map/reshape | solution.py:152
  275.5 7.8 %all-to-all-start.1 = ((bf16[256,16,320]{2,1,0:T(8,128)(2,1)}), bf16[256,16,320]{2,1,0:T(8,128)(2,1)S(1)}, u32[]{:S(2)}, u32[]{:S(2)}) async-start(bf16[256,16,320]{2,1,0:T(8,128)(2,1)} %bitcast.47), calls=%async_computation.1 | async-start | bytes 6291456 | tf_op jit(solution)/shard_map/all_to_all | solution.py:156
  291.4 67.9 %all-to-all-done.1 = bf16[256,16,320]{2,1,0:T(8,128)(2,1)S(1)} async-done(((bf16[256,16,320]{2,1,0:T(8,128)(2,1)}), bf16[256,16,320]{2,1,0:T(8,128)(2,1)S(1)}, u32[]{:S(2)}, u32[]{:S(2)}) %all-to-all-start.1) | async-done | bytes 2621472 | tf_op jit(solution)/shard_map/all_to_all | solution.py:156
  362.0 5.0 %fusion.13 = bf16[4096,320]{1,0:T(8,128)(2,1)S(1)} fusion(bf16[256,16,320]{2,1,0:T(8,128)(2,1)} %gather_fusion, pred[4096]{0:T(1024)(128)(4,1)S(1)} %broadcast_in_dim.141, pred[4096]{0:T(1024)(128)(4,1)S(1)} %broadcast_in_dim.135), kind=kLoop, calls=%fused_computation.21 | loop fusion | flops 2621440 | bytes 5251072 | tf_op jit(solution)/shard_map/vmap(jit(_where))/select_n | solution.py:170
  (76 shorter events, 30.9 us)
Async XLA Ops:
  6.5 88.3 %all-gather.6.cloned.1.call-start = ((), (), s32[]{:S(2)}) async-start(), calls=%async_computation.3 | async-start | bytes 5990400 | tf_op jit(solution)/shard_map/all_gather | solution.py:99
  10.2 249.6 %all-gather.4.cloned.1.call-start = ((), (), s32[]{:S(2)}) async-start(), calls=%async_computation.2 | async-start | bytes 4096000 | tf_op jit(solution)/shard_map/all_gather | solution.py:102
  157.3 23.6 %copy-start = (bf16[4096,320]{1,0:T(8,128)(2,1)}, bf16[4096,320]{1,0:T(8,128)(2,1)S(1)}, u32[]{:S(2)}) copy-start(bf16[4096,320]{1,0:T(8,128)(2,1)S(1)} %copy.55) | copy-start | bytes 7864324
  157.3 6.7 %copy-start.1 = (bf16[4096,640]{1,0:T(8,128)(2,1)S(1)}, bf16[4096,640]{1,0:T(8,128)(2,1)}, u32[]{:S(2)}) copy-start(bf16[4096,640]{1,0:T(8,128)(2,1)} %copy.54) | copy-start | bytes 15728644
  162.7 1.4 copy-start.5
  165.4 2.8 copy-start.6
  166.8 2.7 copy-start.2
  168.2 2.0 copy-start.7
  208.0 41.0 %all-to-all-start = ((bf16[64,4,16,1,320]{4,2,0,3,1:T(8,128)(2,1)}), bf16[64,4,16,1,320]{4,2,0,3,1:T(8,128)(2,1)S(1)}, u32[]{:S(2)}, u32[]{:S(2)}) async-start(bf16[64,4,16,1,320]{4,2,0,3,1:T(8,128)(2,1)} %copy.60), calls=%async_computation | async-start | bytes 6291456 | tf_op jit(solution)/shard_map/all_to_all | solution.py:140
  275.5 7.8 %copy-start.3 = (s32[64]{0:T(128)S(1)}, s32[64]{0:T(128)}, u32[]{:S(2)}) copy-start(s32[64]{0:T(128)} %param.10) | copy-start | bytes 772
  275.5 11.1 %copy-start.4 = (s32[64]{0:T(128)S(1)}, s32[64]{0:T(128)}, u32[]{:S(2)}) copy-start(s32[64]{0:T(128)} %param.9) | copy-start | bytes 772
  275.5 83.8 %all-to-all-start.1 = ((bf16[256,16,320]{2,1,0:T(8,128)(2,1)}), bf16[256,16,320]{2,1,0:T(8,128)(2,1)S(1)}, u32[]{:S(2)}, u32[]{:S(2)}) async-start(bf16[256,16,320]{2,1,0:T(8,128)(2,1)} %bitcast.47), calls=%async_computation.1 | async-start | bytes 6291456 | tf_op jit(solution)/shard_map/all_to_all | solution.py:156
Sparse Core Ops, SparseCore 0:
  10.4 84.3 all-gather.5
  107.3 39.4 all-gather.3

commit v5 on v4

--- a/solution.py
+++ b/solution.py
@@ -136,13 +136,13 @@
         )
     mixed = mixed.astype(jnp.bfloat16)
 
-    spread = mixed.reshape(windows, QUARTERS, quarter_tokens, 1, width)
-    gathered = lax.all_to_all(spread, "mp", split_axis=1, concat_axis=3, tiled=True)
-    gathered = gathered.reshape(windows * quarter_tokens, QUARTERS * width)
-
+    spread = mixed.reshape(windows, QUARTERS, quarter_tokens, width)
+    gathered = lax.all_to_all(spread, "mp", split_axis=1, concat_axis=1, tiled=True)
+    out_grouped = out_full_t.reshape(model_width, QUARTERS, width)
     branch = lax.dot_general(
-        gathered, out_full_t, (((1,), (1,)), ((), ())), preferred_element_type=jnp.float32
+        gathered, out_grouped, (((1, 3), (1, 2)), ((), ())), preferred_element_type=jnp.float32
     )
+    branch = branch.reshape(windows * quarter_tokens, model_width)
     residual = patches.reshape(windows, QUARTERS, quarter_tokens, model_width)
     residual = lax.dynamic_index_in_dim(residual, mp_index, 1, keepdims=False)
     residual = residual.reshape(windows * quarter_tokens, model_width).astype(jnp.float32)

time: 382 us -> 357 us (0.935); the launches traced: 377 us -> 356 us
  local copies, waits for them, and re-layouts: 64.9 us -> 54 us
  matrix products: 76.2 us -> 66.5 us
    dot_general x4, matrix products: 35.8 us -> 26 us  [local(): jnp.einsum('wqk,wkd->wqd', weights, own_values, preferred_element_type=jn...]
    all_to_all x1 -> x0, local copies, waits for them, and re-layouts: 5.71 us -> none  [local(): lax.all_to_all(spread, 'mp', split_axis=1, concat_axis=3, tiled=True)]
    reshape x2 -> x1, local copies, waits for them, and re-layouts: 7.12 us -> 1.98 us  [local(): spread = mixed.reshape(windows, QUARTERS, quarter_tokens, width)]
  transfers between devices with their start and end apart: 4 -> 4, of which waited for: 3 -> 3; matrix products, arithmetic and copies ran while one was open for 35% -> 31% of each run, Pallas kernels for 0% -> 0%
where the time goes in v5:
time: 357 us; the launch traced here: 356 us
  waiting for transfers between devices  173 us (48%)
  matrix products  66.5 us (19%)
  local copies, waits for them, and re-layouts  54 us (15%)
  other arithmetic  31.8 us (9%)
  between operations  18.9 us (5%)
  starting transfers between devices  11.7 us (3%)
    all_gather x1, waiting for transfers between devices, local(): joined = lax.all_gather(fused_rows, 'seq', axis=0, tiled=True)  71.3 us
    all_to_all x1, waiting for transfers between devices, local(): lax.all_to_all(sectioned, ('seq', 'mp'), split_axis=0, concat_axis=0, til...  67.9 us
    all_to_all x1, waiting for transfers between devices, local(): lax.all_to_all(spread, 'mp', split_axis=1, concat_axis=1, tiled=True)  33.7 us
    dot_general x4, matrix products, local(): jnp.einsum('wqk,wkd->wqd', weights, own_values, preferred_element_type=jn...  26 us
    dot_general x1, matrix products, local(): projected = jnp.dot(normed, fused, preferred_element_type=jnp.float32)  23.8 us
    convert_element_type x1, other arithmetic, local(): turned.astype(jnp.bfloat16).reshape(windows, window_tokens, 2 * width)  10.4 us
    dot_general x4, matrix products, local(): jnp.einsum('wqd,wkd->wqk', picked, key_block, preferred_element_type=jnp....  9.45 us
    reshape x2, local copies, waits for them, and re-layouts, local(): block_out.reshape(page_count, quarter_tokens, QUARTERS, share_width)  8.5 us
  transfers between devices with their start and end apart: 4, of which 3 were waited for; matrix products, arithmetic and copies ran while one was open for 31% of the time, Pallas kernels for 0%

profile of v5, /device:TPU:1, one launch (start us, length us, event | category | flops | bytes accessed | tf_op | source)
XLA Modules:
  0.0 355.9 jit_solution(10992189034661572990)
XLA Ops:
  12.5 6.1 %fusion.4 = f32[4096]{0:T(1024)S(1)} fusion(bf16[4096,1280]{1,0:T(8,128)(2,1)} %param.6), kind=kLoop, calls=%fused_computation.7 | loop fusion | flops 15724544 | bytes 10502144 | tf_op jit(solution)/shard_map/reduce_sum | solution.py:62
  18.7 4.8 %fusion.69 = (f32[4096,80]{0,1:T(8,128)S(1)}, f32[4096,80]{0,1:T(8,128)S(1)}) fusion(f32[4096,20]{0,1:T(8,128)S(1)} %get-tuple-element.19, f32[4096,20]{0,1:T(8,128)S(1)} %get-tuple-element.18), kind=kLoop, calls=%fused_computation.88 | loop fusion | flops 983040 | bytes 3276800 | tf_op jit(solution)/shard_map/cos | solution.py:25
  23.5 71.3 %all-gather.6.cloned.1.call-done = bf16[64,20,1920]{2,1,0:T(8,128)(2,1)} async-done(((bf16[1,20,1920]{2,1,0:T(8,128)(2,1)}), bf16[64,20,1920]{2,1,0:T(8,128)(2,1)}) %all-gather.6.cloned.1.call-update) | async-done | bytes 4915216 | tf_op jit(solution)/shard_map/all_gather | solution.py:99
  94.8 7.5 %reshape.662 = bf16[1280,1920]{1,0:T(8,128)(2,1)} reshape(bf16[64,20,1920]{2,1,0:T(8,128)(2,1)} %all-gather.6.cloned.1.call-done) | data formatting | bytes 9830400
  107.2 23.8 %fusion.6 = f32[4096,1600]{0,1:T(8,128)} fusion(bf16[4096,1280]{1,0:T(8,128)(2,1)} %param.6, f32[4096]{0:T(1024)S(1)} %add_rsqrt_fusion, bf16[1280,1920]{1,0:T(8,128)(2,1)} %reshape.662), kind=kOutput, calls=%fused_computation.9 | convolution fusion | flops 16792944640 | bytes 40976384 | tf_op jit(solution)/shard_map/dot_general | solution.py:113
  131.0 4.4 %slice.125 = bf16[4096,320]{0,1:T(8,128)(2,1)} slice(f32[4096,1600]{0,1:T(8,128)} %fusion.6), slice={[0:4096], [1280:1600]} | slice | bytes 5242880 | tf_op jit(solution)/shard_map/slice | solution.py:119
  135.4 10.4 %fusion.9 = bf16[4096,640]{0,1:T(8,128)(2,1)} fusion(f32[4096,1600]{0,1:T(8,128)} %fusion.6, f32[4096,80]{0,1:T(8,128)S(1)} %get-tuple-element.11, f32[4096,80]{0,1:T(8,128)S(1)} %get-tuple-element.10), kind=kLoop, calls=%fused_computation.12 | loop fusion | flops 10485760 | bytes 28835840 | tf_op jit(solution)/shard_map/convert_element_type | solution.py:116
  145.8 7.9 %copy.60 = bf16[4096,640]{1,0:T(8,128)(2,1)} copy(bf16[4096,640]{0,1:T(8,128)(2,1)} %fusion.9) | data formatting | bytes 10485760 | tf_op jit(solution)/shard_map/convert_element_type | solution.py:116
  153.7 3.5 copy.61
  157.2 5.4 %fusion.20 = f32[64,64,64]{1,2,0:T(8,128)S(1)} fusion(pred[320]{0:T(512)(128)(4,1)S(1)} %broadcast_compare_fusion.1, bf16[64,64,640]{2,1,0:T(8,128)(2,1)} %bitcast.54), kind=kOutput, calls=%fused_computation.28 | convolution fusion | flops 169082880 | bytes 7340352 | tf_op jit(solution)/shard_map/wqd,wkd->wqk/dot_general | solution.py:127
  170.1 5.4 %fusion.22 = f32[64,64,320]{2,1,0:T(8,128)} fusion(bf16[64,64,320]{2,1,0:T(8,128)(2,1)S(1)} %bitcast.50, pred[320]{0:T(512)(128)(4,1)S(1)} %broadcast_compare_fusion.3, f32[64,64]{1,0:T(8,128)S(1)} %fusion.127, f32[64,64,64]{1,2,0:T(8,128)} %copy-done.7), kind=kOutput, calls=%fused_computation.30 | convolution fusion | flops 170135616 | bytes 8929600 | tf_op jit(solution)/shard_map/wqk,wkd->wqd/dot_general | solution.py:134
  175.5 5.4 %fusion.14 = f32[64,64,320]{2,1,0:T(8,128)} fusion(bf16[64,64,320]{2,1,0:T(8,128)(2,1)S(1)} %bitcast.51, pred[320]{0:T(512)(128)(4,1)S(1)} %broadcast_compare_fusion, f32[64,64]{1,0:T(8,128)S(1)} %fusion.125, f32[64,64,64]{1,2,0:T(8,128)} %copy-done.6), kind=kOutput, calls=%fused_computation.22 | convolution fusion | flops 170135616 | bytes 8929600 | tf_op jit(solution)/shard_map/wqk,wkd->wqd/dot_general | solution.py:134
  180.9 5.3 %fusion.18 = f32[64,64,320]{2,1,0:T(8,128)} fusion(bf16[64,64,320]{2,1,0:T(8,128)(2,1)S(1)} %bitcast.52, pred[320]{0:T(512)(128)(4,1)S(1)} %broadcast_compare_fusion.1, f32[64,64]{1,0:T(8,128)S(1)} %fusion.126, f32[64,64,64]{1,2,0:T(8,128)} %copy-done.5), kind=kOutput, calls=%fused_computation.26 | convolution fusion | flops 170135616 | bytes 8929600 | tf_op jit(solution)/shard_map/wqk,wkd->wqd/dot_general | solution.py:134
  186.2 9.9 %add_convert_fusion = bf16[64,64,320]{2,1,0:T(8,128)(2,1)S(1)} fusion(f32[64,64,320]{2,1,0:T(8,128)} %fusion.14, f32[64,64,320]{2,1,0:T(8,128)} %fusion.18, f32[64,64,320]{2,1,0:T(8,128)} %fusion.22, bf16[64,64,320]{2,1,0:T(8,128)(2,1)} %bitcast.53, pred[320]{0:T(512)(128)(4,1)S(1)} %broadcast_compare_fusion.2, f32[64,64]{1,0:T(8,128)S(1)} %fusion.128, ...), kind=kOutput, calls=%fused_computation.15 | convolution fusion | flops 175378496 | bytes 22036800 | tf_op jit(solution)/shard_map/wqk,wkd->wqd/dot_general | solution.py:134
  198.1 3.9 %all-to-all-start = ((bf16[64,4,16,320]{3,2,0,1:T(8,128)(2,1)}), bf16[64,4,16,320]{3,2,0,1:T(8,128)(2,1)S(1)}, u32[]{:S(2)}, u32[]{:S(2)}) async-start(bf16[64,4,16,320]{3,2,0,1:T(8,128)(2,1)} %copy.66), calls=%async_computation | async-start | bytes 6291456 | tf_op jit(solution)/shard_map/all_to_all | solution.py:140
  201.9 3.4 constant_dynamic-slice_fusion
  205.4 33.7 %all-to-all-done = bf16[64,4,16,320]{3,2,0,1:T(8,128)(2,1)S(1)} async-done(((bf16[64,4,16,320]{3,2,0,1:T(8,128)(2,1)}), bf16[64,4,16,320]{3,2,0,1:T(8,128)(2,1)S(1)}, u32[]{:S(2)}, u32[]{:S(2)}) %all-to-all-start) | async-done | bytes 2621472 | tf_op jit(solution)/shard_map/all_to_all | solution.py:140
  239.0 7.3 %fusion.11 = bf16[1024,1280]{1,0:T(8,128)(2,1)} fusion(bf16[1024,1280]{1,0:T(8,128)(2,1)} %bitcast.59, bf16[1024,4,320]{2,0,1:T(8,128)(2,1)S(1)} %bitcast.58, bf16[1280,4,320]{0,2,1:T(8,128)(2,1)} %bitcast.63), kind=kOutput, calls=%fused_computation.18 | convolution fusion | flops 3359375360 | bytes 11141120 | tf_op jit(solution)/shard_map/dot_general | solution.py:142
  246.3 6.1 %reshape.648 = bf16[64,16,4,320]{3,2,1,0:T(4,128)(2,1)S(1)} reshape(bf16[1024,1280]{1,0:T(8,128)(2,1)} %fusion.11) | data formatting | bytes 5242880 | tf_op jit(solution)/shard_map/reshape | solution.py:152
  254.8 7.8 %all-to-all-start.1 = ((bf16[256,16,320]{2,1,0:T(8,128)(2,1)}), bf16[256,16,320]{2,1,0:T(8,128)(2,1)S(1)}, u32[]{:S(2)}, u32[]{:S(2)}) async-start(bf16[256,16,320]{2,1,0:T(8,128)(2,1)} %bitcast.48), calls=%async_computation.1 | async-start | bytes 6291456 | tf_op jit(solution)/shard_map/all_to_all | solution.py:156
  270.6 67.9 %all-to-all-done.1 = bf16[256,16,320]{2,1,0:T(8,128)(2,1)S(1)} async-done(((bf16[256,16,320]{2,1,0:T(8,128)(2,1)}), bf16[256,16,320]{2,1,0:T(8,128)(2,1)S(1)}, u32[]{:S(2)}, u32[]{:S(2)}) %all-to-all-start.1) | async-done | bytes 2621472 | tf_op jit(solution)/shard_map/all_to_all | solution.py:156
  338.6 2.7 gather_fusion
  341.3 5.0 %fusion.13 = bf16[4096,320]{1,0:T(8,128)(2,1)S(1)} fusion(bf16[256,16,320]{2,1,0:T(8,128)(2,1)} %gather_fusion, pred[4096]{0:T(1024)(128)(4,1)S(1)} %broadcast_in_dim.141, pred[4096]{0:T(1024)(128)(4,1)S(1)} %broadcast_in_dim.135), kind=kLoop, calls=%fused_computation.21 | loop fusion | flops 2621440 | bytes 5251072 | tf_op jit(solution)/shard_map/vmap(jit(_where))/select_n | solution.py:170
  346.3 2.7 copy.70
  (74 shorter events, 25.4 us)
Async XLA Ops:
  6.5 88.3 %all-gather.6.cloned.1.call-start = ((), (), s32[]{:S(2)}) async-start(), calls=%async_computation.3 | async-start | bytes 5990400 | tf_op jit(solution)/shard_map/all_gather | solution.py:99
  10.2 228.8 %all-gather.4.cloned.1.call-start = ((), (), s32[]{:S(2)}) async-start(), calls=%async_computation.2 | async-start | bytes 4096000 | tf_op jit(solution)/shard_map/all_gather | solution.py:102
  157.2 23.6 %copy-start = (bf16[4096,320]{1,0:T(8,128)(2,1)}, bf16[4096,320]{1,0:T(8,128)(2,1)S(1)}, u32[]{:S(2)}) copy-start(bf16[4096,320]{1,0:T(8,128)(2,1)S(1)} %copy.61) | copy-start | bytes 7864324
  157.2 6.7 %copy-start.1 = (bf16[4096,640]{1,0:T(8,128)(2,1)S(1)}, bf16[4096,640]{1,0:T(8,128)(2,1)}, u32[]{:S(2)}) copy-start(bf16[4096,640]{1,0:T(8,128)(2,1)} %copy.60) | copy-start | bytes 15728644
  162.6 1.4 copy-start.5
  165.3 2.8 copy-start.6
  166.7 2.7 copy-start.2
  168.1 2.0 copy-start.7
  198.1 41.0 %all-to-all-start = ((bf16[64,4,16,320]{3,2,0,1:T(8,128)(2,1)}), bf16[64,4,16,320]{3,2,0,1:T(8,128)(2,1)S(1)}, u32[]{:S(2)}, u32[]{:S(2)}) async-start(bf16[64,4,16,320]{3,2,0,1:T(8,128)(2,1)} %copy.66), calls=%async_computation | async-start | bytes 6291456 | tf_op jit(solution)/shard_map/all_to_all | solution.py:140
  254.8 7.8 %copy-start.3 = (s32[64]{0:T(128)S(1)}, s32[64]{0:T(128)}, u32[]{:S(2)}) copy-start(s32[64]{0:T(128)} %param.10) | copy-start | bytes 772
  254.8 11.0 %copy-start.4 = (s32[64]{0:T(128)S(1)}, s32[64]{0:T(128)}, u32[]{:S(2)}) copy-start(s32[64]{0:T(128)} %param.9) | copy-start | bytes 772
  254.8 83.8 %all-to-all-start.1 = ((bf16[256,16,320]{2,1,0:T(8,128)(2,1)}), bf16[256,16,320]{2,1,0:T(8,128)(2,1)S(1)}, u32[]{:S(2)}, u32[]{:S(2)}) async-start(bf16[256,16,320]{2,1,0:T(8,128)(2,1)} %bitcast.48), calls=%async_computation.1 | async-start | bytes 6291456 | tf_op jit(solution)/shard_map/all_to_all | solution.py:156
Sparse Core Ops, SparseCore 0:
  10.4 84.3 all-gather.5
  107.3 39.4 all-gather.3
